TPU v7x, 32 devices: a whole 2x2x4 slice. The times are simulated.
32 devices in a mesh: groups: 2 (over x), chan: 16 (over z, y, core).
Axes of the slice: x: 2, y: 2, z: 4, core: 2. Of those that a mesh axis runs over, the one named last changes fastest.
Arguments:
- sky_data: bfloat16 [1024, 512, 2, 256], P('groups', 'chan'), parts along dimension 0, may hold values from -1.1953125 to 1.1953125
- beam_gains: bfloat16 [1024, 512, 256], P('groups', 'chan'), parts along dimension 0, may hold values from 0.099609375 to 1
- mixing: float32 [1024, 4], P(('groups', 'chan')), parts along dimension 0, may hold values from -0.25 to 0.25
- noise_levels: int32 [512], P('chan'), may hold values from 1 to 16
- threshold_levels: int32 [4, 2], replicated, may hold values from 1 to 8
- start_sources: float32 [1024, 4, 256], P(('groups', 'chan')), parts along dimension 0, may hold values from -6 to 6
Outputs:
- sources: float32 [1024, 4, 256], P(('groups', 'chan')), parts along dimension 0
There are 2 independent parts, one for each index of `groups`. A program takes and returns all parts, laid end to end along the dimension named above; an argument that names none is the same for every part. Nothing has to cross between parts.
All inputs are finite; a program needn't handle non-finite values.
Results may differ from a plain program's by a relative error of at most 0.025.
Values may be sent and summed in bfloat16 or wider, within the bound.
No kernel may reach another device: no remote copies, remote signals or barrier semaphores. Data moves between devices by JAX's collectives and lax.ppermute only.
A program may use at most 128 MiB of HBM per device.

v0:
```python
import math

import jax
import jax.numpy as jnp
from jax import lax
from jax.sharding import PartitionSpec as P

ITERS = 2


def padded_2(cells, sides, width):
    for axis, dim in sides:
        count = lax.axis_size(axis)
        ends = count - 1
        head = lax.slice_in_dim(cells, 0, width, axis=dim)
        tail = lax.slice_in_dim(cells, cells.shape[dim] - width, cells.shape[dim], axis=dim)
        cells = jnp.concatenate(
            [
                lax.ppermute(tail, axis, [(i, (i + 1) % count) for i in range(ends)]),
                cells,
                lax.ppermute(head, axis, [((i + 1) % count, i) for i in range(ends)]),
            ],
            axis=dim,
        )
    return cells


def gather_rows(strip, axis):
    count = lax.axis_size(axis)
    bits = count.bit_length() - 1
    assert 1 << bits == count
    own = lax.axis_index(axis)
    joined = strip
    for depth, bit in enumerate(reversed(range(bits))):
        partner = lax.ppermute(joined, axis, [(i, i ^ (1 << bit)) for i in range(count)])
        upper = ((own >> bit) & 1) == 1
        low = jnp.where(upper, partner, joined)
        high = jnp.where(upper, joined, partner)
        joined = jnp.stack([low, high], axis=depth)
    return joined.reshape((count * strip.shape[0],) + strip.shape[1:])


def sum_rows(values, axis):
    count = lax.axis_size(axis)
    chunks = values.reshape((count, values.shape[0] // count) + values.shape[1:])
    received = lax.all_to_all(chunks.astype(jnp.bfloat16), axis, 0, 0, tiled=True)
    return received.astype(jnp.float32).sum(axis=0)


def dft_tables(length):
    positions = jnp.arange(length, dtype=jnp.int32)
    angles = (positions[:, None] * positions[None, :] % length).astype(jnp.float32) * (
        2.0 * math.pi / length
    )
    norm_factor = 1.0 / math.sqrt(length)
    return (
        (jnp.cos(angles) * norm_factor).astype(jnp.bfloat16),
        (-jnp.sin(angles) * norm_factor).astype(jnp.bfloat16),
    )


def column_part(rounded, col_cat):
    row_count, source_count, col_count = rounded.shape
    product = jnp.dot(
        rounded.reshape(row_count * source_count, col_count),
        col_cat,
        preferred_element_type=jnp.float32,
    )
    return product.astype(jnp.bfloat16).reshape(row_count, source_count * 2 * col_count)


def combine_forward(real_prod, imag_prod, source_count, col_count):
    real_prod = real_prod.reshape(real_prod.shape[0], source_count, 2, col_count)
    imag_prod = imag_prod.reshape(imag_prod.shape[0], source_count, 2, col_count)
    real_out = real_prod[:, :, 0] - imag_prod[:, :, 1]
    imag_out = real_prod[:, :, 1] + imag_prod[:, :, 0]
    return jnp.stack([real_out, imag_out], axis=2)


def inverse_rows(row_real, row_imag, packed_grad, col_back, source_count, col_count):
    real_prod = jnp.dot(row_real, packed_grad, preferred_element_type=jnp.float32)
    imag_prod = jnp.dot(row_imag, packed_grad, preferred_element_type=jnp.float32)
    real_prod = real_prod.reshape(real_prod.shape[0], source_count, 2, col_count)
    imag_prod = imag_prod.reshape(imag_prod.shape[0], source_count, 2, col_count)
    real_out = real_prod[:, :, 0] + imag_prod[:, :, 1]
    imag_out = real_prod[:, :, 1] - imag_prod[:, :, 0]
    joined = jnp.concatenate([real_out, imag_out], axis=-1).astype(jnp.bfloat16)
    result = jnp.dot(
        joined.reshape(-1, 2 * col_count), col_back, preferred_element_type=jnp.float32
    )
    return result.reshape(real_prod.shape[0], source_count, col_count)


def block_gradient(fourier, data_block, beam_block, mix_block, level_block):
    predicted = jnp.einsum("ct,ktzl->kczl", mix_block, fourier)
    beam_gain = beam_block.astype(jnp.float32)[:, :, None, :]
    residual = data_block.astype(jnp.float32) - beam_gain * predicted
    weight = level_block.astype(jnp.float32) * 0.25
    weighted = weight[None, :, None, None] * beam_gain * residual
    summed = jnp.einsum("cs,kczl->kszl", mix_block, weighted)
    return summed.astype(jnp.bfloat16)


def smooth_rows(padded, spacing, row_count):
    return (
        padded[0:row_count]
        + 2.0 * padded[spacing : spacing + row_count]
        + padded[2 * spacing : 2 * spacing + row_count]
    ) * 0.25


def smooth_cols(values, spacing):
    padded = jnp.pad(values, ((0, 0), (0, 0), (spacing, spacing)))
    return (
        padded[..., : -2 * spacing]
        + 2.0 * padded[..., spacing:-spacing]
        + padded[..., 2 * spacing :]
    ) * 0.25


def shrink(values, bound_value):
    return values - jnp.clip(values, -bound_value, bound_value)


def combine_scales(updated, smooth_one, coarse, fine_bound, coarse_bound):
    return (
        coarse
        + shrink(smooth_one - coarse, coarse_bound)
        + shrink(updated - smooth_one, fine_bound)
    )


def body(sky_data, beam_gains, mixing, noise_levels, threshold_levels, start_sources):
    strip_rows, source_count, col_count = start_sources.shape
    full_rows = strip_rows * lax.axis_size("chan")
    row_real, row_imag = dft_tables(full_rows)
    col_real, col_imag = dft_tables(col_count)
    col_cat = jnp.concatenate([col_real, col_imag], axis=1)
    col_back = jnp.concatenate([col_real, col_imag], axis=0)
    bounds = threshold_levels.astype(jnp.float32) * 0.05
    fine_bound = bounds[:, 0][:, None]
    coarse_bound = bounds[:, 1][:, None]
    sources = start_sources
    for iteration in range(ITERS):
        rounded = sources.astype(jnp.bfloat16)
        gathered = gather_rows(rounded, "chan")
        packed = column_part(gathered, col_cat)
        fourier = combine_forward(
            jnp.dot(row_real, packed, preferred_element_type=jnp.float32),
            jnp.dot(row_imag, packed, preferred_element_type=jnp.float32),
            source_count,
            col_count,
        )
        grad_local = block_gradient(fourier, sky_data, beam_gains, mixing, noise_levels)
        packed_grad = grad_local.reshape(full_rows, source_count * 2 * col_count)
        gradient = sum_rows(
            inverse_rows(row_real, row_imag, packed_grad, col_back, source_count, col_count),
            "chan",
        )
        updated = sources + gradient
        fine_pad = padded_2(updated, (("chan", 0),), 1)
        smooth_one = smooth_cols(smooth_rows(fine_pad, 1, strip_rows), 1)
        coarse_pad = padded_2(smooth_one, (("chan", 0),), 2)
        coarse = smooth_cols(smooth_rows(coarse_pad, 2, strip_rows), 2)
        sources = combine_scales(updated, smooth_one, coarse, fine_bound, coarse_bound)
    return sources


def solution(mesh):
    return jax.shard_map(
        body,
        mesh=mesh,
        in_specs=(
            P("groups", "chan", None, None),
            P("groups", "chan", None),
            P(("groups", "chan"), None),
            P("chan"),
            P(),
            P(("groups", "chan"), None, None),
        ),
        out_specs=P(("groups", "chan"), None, None),
        check_vma=False,
    )
```

profile of v0, /device:TPU:1, one launch (start us, length us, event | category | flops | bytes accessed | tf_op | source)
XLA Modules:
  0.0 285.8 jit_solution(15246172114744807673)
XLA Ops:
  0.9 3.2 %collective-permute-start = (bf16[32,4,256]{2,0,1:T(8,128)(2,1)S(1)}, bf16[32,4,256]{2,0,1:T(8,128)(2,1)S(1)}, u32[]{:S(2)}, u32[]{:S(2)}) collective-permute-start(bf16[32,4,256]{2,0,1:T(8,128)(2,1)S(1)} %copy.81), channel_id=1, source_target_pairs={{0,8},{1,9},{2,10},{3,11},{4,12},{5,13},{6,14},{7,15},{8,0},{9,1},... | collective-permute-start | bytes 196616 | tf_op jit(solution)/shard_map/ppermute | solution.py:35
  13.4 3.3 %collective-permute-done.2 = bf16[2,2,32,4,256]{4,2,3,0,1:T(8,128)(2,1)S(1)} collective-permute-done((bf16[2,2,32,4,256]{4,2,3,0,1:T(8,128)(2,1)S(1)}, bf16[2,2,32,4,256]{4,2,3,0,1:T(8,128)(2,1)S(1)}, u32[]{:S(2)}, u32[]{:S(2)}) %collective-permute-start.2) | collective-permute-done | bytes 262176 | tf_op jit(solution)/shard_map/ppermute | solution.py:35
  16.9 4.5 %collective-permute-start.3 = (bf16[2,2,2,32,4,256]{5,3,4,0,1,2:T(8,128)(2,1)S(1)}, bf16[2,2,2,32,4,256]{5,3,4,0,1,2:T(8,128)(2,1)S(1)}, u32[]{:S(2)}, u32[]{:S(2)}) collective-permute-start(bf16[2,2,2,32,4,256]{5,3,4,0,1,2:T(8,128)(2,1)S(1)} %pad_maximum_fusion.6), channel_id=1, source_target_pairs={{0,1},{1,0},{2,3},{3,2},{4,5},{5,4},{6,7},{7,6},{8,9},{9,8},{10,11... | collective-permute-start | bytes 1572872 | tf_op jit(solution)/shard_map/ppermute | solution.py:35
  21.4 11.7 %broadcast_multiply_fusion = f32[512,32,256]{2,1,0:T(8,128)} fusion(f32[32]{0:T(128)S(1)} %convert_multiply_fusion.1, bf16[512,32,256]{2,1,0:T(8,128)(2,1)} %param.7), kind=kLoop, calls=%fused_computation.16 | loop fusion | flops 8388608 | bytes 25165952 | tf_op jit(solution)/shard_map/mul | solution.py:99
  33.1 11.3 %convert_element_type.120 = f32[512,32,256]{2,1,0:T(8,128)} convert(bf16[512,32,256]{2,1,0:T(8,128)(2,1)} %param.7) | non-fusion elementwise | flops 4194304 | bytes 25165824 | tf_op jit(solution)/shard_map/convert_element_type | solution.py:96
  50.2 3.1 %copy.30 = bf16[2048,512]{1,0:T(8,128)(2,1)S(1)} copy(bf16[2048,512]{0,1:T(8,128)(2,1)} %bitcast.121) | data formatting | bytes 4194304 | tf_op jit(solution)/shard_map/dot_general | solution.py:149
  53.3 4.9 %fusion.62 = f32[512,4,2,256]{3,0,2,1:T(8,128)S(1)} fusion(bf16[4,2,256,512]{3,2,1,0:T(8,128)(2,1)S(1)} %bitcast.123), kind=kOutput, calls=%fused_computation.77 | convolution fusion | flops 1078198272 | bytes 6291456 | tf_op jit(solution)/shard_map/dot_general | solution.py:150
  58.3 4.9 %fusion.68 = f32[512,4,2,256]{3,0,2,1:T(8,128)S(1)} fusion(bf16[4,2,256,512]{3,2,1,0:T(8,128)(2,1)S(1)} %bitcast.124), kind=kOutput, calls=%fused_computation.79 | convolution fusion | flops 1077936128 | bytes 6291456 | tf_op jit(solution)/shard_map/dot_general | solution.py:149
  64.7 23.7 %convert_bitcast_fusion.1 = bf16[512,4,2,256]{3,1,2,0:T(4,128)(2,1)} fusion(f32[512,32,256]{2,1,0:T(8,128)} %convert_element_type.120, f32[512,32,256]{2,1,0:T(8,128)} %broadcast_multiply_fusion, bf16[512,32,2,256]{3,2,1,0:T(2,128)(2,1)} %param.6, bf16[512,4,2,256]{3,0,2,1:T(8,128)(2,1)S(1)} %pad_maximum_fusion, f32[32,4]{0,1:T(4,128)S(1)} %copy-done.1), kind=kOutput, calls=%fused_computation.52 | convolution fusion | flops 176160896 | bytes 54526464 | tf_op jit(solution)/shard_map/cs,kczl->kszl/dot_general | solution.py:100
  88.4 12.8 %copy.32 = bf16[512,4,2,256]{0,3,2,1:T(8,128)(2,1)S(1)} copy(bf16[512,4,2,256]{3,1,2,0:T(4,128)(2,1)} %convert_bitcast_fusion.1) | data formatting | bytes 4194304 | tf_op jit(solution)/shard_map/convert_element_type | solution.py:101
  101.3 4.9 %fusion.32 = f32[512,4,2,256]{3,0,2,1:T(8,128)S(1)} fusion(bf16[512,4,2,256]{0,3,2,1:T(8,128)(2,1)S(1)} %copy.32), kind=kOutput, calls=%fused_computation.45 | convolution fusion | flops 1078198272 | bytes 6291456 | tf_op jit(solution)/shard_map/dot_general | solution.py:82
  106.2 4.9 %fusion.34 = f32[512,4,2,256]{3,0,2,1:T(8,128)S(1)} fusion(bf16[512,4,2,256]{0,3,2,1:T(8,128)(2,1)S(1)} %copy.32), kind=kOutput, calls=%fused_computation.47 | convolution fusion | flops 1077936128 | bytes 6291456 | tf_op jit(solution)/shard_map/dot_general | solution.py:81
  112.8 31.6 %all_to_all.10 = bf16[16,32,4,256]{3,1,2,0:T(8,128)(2,1)S(1)} all-to-all(bf16[16,32,4,256]{3,1,2,0:T(8,128)(2,1)S(1)} %fusion.44), channel_id=1, replica_groups=mesh['groups'=2,'chan'=16] {'chan'}, dimensions={0} | all-to-all | bytes 2097152 | tf_op jit(solution)/shard_map/all_to_all | solution.py:46
  156.7 4.0 %collective-permute-done.7 = f32[2,4,256]{2,0,1:T(2,128)S(1)} collective-permute-done((f32[2,4,256]{2,0,1:T(2,128)S(1)}, f32[2,4,256]{2,0,1:T(2,128)S(1)}, u32[]{:S(2)}, u32[]{:S(2)}) %collective-permute-start.7) | collective-permute-done | bytes 8224 | tf_op jit(solution)/shard_map/ppermute | solution.py:21
  161.5 4.3 %collective-permute-done.8 = bf16[32,4,256]{2,0,1:T(8,128)(2,1)S(1)} collective-permute-done((bf16[32,4,256]{2,0,1:T(8,128)(2,1)S(1)}, bf16[32,4,256]{2,0,1:T(8,128)(2,1)S(1)}, u32[]{:S(2)}, u32[]{:S(2)}) %collective-permute-start.8) | collective-permute-done | bytes 65568 | tf_op jit(solution)/shard_map/ppermute | solution.py:35
  172.2 5.2 %collective-permute-done.10 = bf16[2,2,32,4,256]{4,2,3,0,1:T(8,128)(2,1)S(1)} collective-permute-done((bf16[2,2,32,4,256]{4,2,3,0,1:T(8,128)(2,1)S(1)}, bf16[2,2,32,4,256]{4,2,3,0,1:T(8,128)(2,1)S(1)}, u32[]{:S(2)}, u32[]{:S(2)}) %collective-permute-start.10) | collective-permute-done | bytes 262176 | tf_op jit(solution)/shard_map/ppermute | solution.py:35
  189.1 4.9 %fusion.59 = f32[512,4,2,256]{3,0,2,1:T(8,128)S(1)} fusion(bf16[4,2,256,512]{3,2,1,0:T(8,128)(2,1)S(1)} %bitcast.125), kind=kOutput, calls=%fused_computation.76 | convolution fusion | flops 1078198272 | bytes 6291456 | tf_op jit(solution)/shard_map/dot_general | solution.py:150
  194.0 4.9 %fusion.65 = f32[512,4,2,256]{3,0,2,1:T(8,128)S(1)} fusion(bf16[4,2,256,512]{3,2,1,0:T(8,128)(2,1)S(1)} %bitcast.126), kind=kOutput, calls=%fused_computation.78 | convolution fusion | flops 1077936128 | bytes 6291456 | tf_op jit(solution)/shard_map/dot_general | solution.py:149
  200.0 23.9 %convert_bitcast_fusion = bf16[512,4,2,256]{3,1,2,0:T(4,128)(2,1)} fusion(f32[512,32,256]{2,1,0:T(8,128)} %convert_element_type.120, f32[512,32,256]{2,1,0:T(8,128)} %broadcast_multiply_fusion, bf16[512,32,2,256]{3,2,1,0:T(2,128)(2,1)} %param.6, bf16[512,4,2,256]{3,0,2,1:T(8,128)(2,1)S(1)} %pad_maximum_fusion.1, f32[32,4]{0,1:T(4,128)S(1)} %copy-done.1), kind=kOutput, calls=%fused_computation.50 | convolution fusion | flops 176160896 | bytes 54526464 | tf_op jit(solution)/shard_map/cs,kczl->kszl/dot_general | solution.py:100
  226.9 4.9 %fusion.26 = f32[512,4,2,256]{3,0,2,1:T(8,128)S(1)} fusion(bf16[512,4,2,256]{0,3,2,1:T(8,128)(2,1)S(1)} %copy.39), kind=kOutput, calls=%fused_computation.39 | convolution fusion | flops 1078198272 | bytes 6291456 | tf_op jit(solution)/shard_map/dot_general | solution.py:82
  231.8 4.9 %fusion.28 = f32[512,4,2,256]{3,0,2,1:T(8,128)S(1)} fusion(bf16[512,4,2,256]{0,3,2,1:T(8,128)(2,1)S(1)} %copy.39), kind=kOutput, calls=%fused_computation.41 | convolution fusion | flops 1077936128 | bytes 6291456 | tf_op jit(solution)/shard_map/dot_general | solution.py:81
  238.4 30.1 %all_to_all.11 = bf16[16,32,4,256]{3,1,2,0:T(8,128)(2,1)S(1)} all-to-all(bf16[16,32,4,256]{3,1,2,0:T(8,128)(2,1)S(1)} %fusion.47), channel_id=1, replica_groups=mesh['groups'=2,'chan'=16] {'chan'}, dimensions={0} | all-to-all | bytes 2097152 | tf_op jit(solution)/shard_map/all_to_all | solution.py:46
  273.1 3.0 %collective-permute-done.13 = f32[1,4,256]{2,0,1:T(1,128)S(1)} collective-permute-done((f32[1,4,256]{2,0,1:T(1,128)S(1)}, f32[1,4,256]{2,0,1:T(1,128)S(1)}, u32[]{:S(2)}, u32[]{:S(2)}) %collective-permute-start.13) | collective-permute-done | bytes 4128 | tf_op jit(solution)/shard_map/ppermute | solution.py:21
  280.7 4.0 %collective-permute-done.15 = f32[2,4,256]{2,0,1:T(2,128)S(1)} collective-permute-done((f32[2,4,256]{2,0,1:T(2,128)S(1)}, f32[2,4,256]{2,0,1:T(2,128)S(1)}, u32[]{:S(2)}, u32[]{:S(2)}) %collective-permute-start.15) | collective-permute-done | bytes 8224 | tf_op jit(solution)/shard_map/ppermute | solution.py:21
  (90 shorter events, 66.4 us)
Async XLA Ops:
  0.9 4.9 %collective-permute-start = (bf16[32,4,256]{2,0,1:T(8,128)(2,1)S(1)}, bf16[32,4,256]{2,0,1:T(8,128)(2,1)S(1)}, u32[]{:S(2)}, u32[]{:S(2)}) collective-permute-start(bf16[32,4,256]{2,0,1:T(8,128)(2,1)S(1)} %copy.81), channel_id=1, source_target_pairs={{0,8},{1,9},{2,10},{3,11},{4,12},{5,13},{6,14},{7,15},{8,0},{9,1},... | collective-permute-start | bytes 196616 | tf_op jit(solution)/shard_map/ppermute | solution.py:35
  6.7 4.7 %collective-permute-start.1 = (bf16[2,32,4,256]{3,1,2,0:T(8,128)(2,1)S(1)}, bf16[2,32,4,256]{3,1,2,0:T(8,128)(2,1)S(1)}, u32[]{:S(2)}, u32[]{:S(2)}) collective-permute-start(bf16[2,32,4,256]{3,1,2,0:T(8,128)(2,1)S(1)} %pad_maximum_fusion.21), channel_id=1, source_target_pairs={{0,4},{1,5},{2,6},{3,7},{4,0},{5,1},{6,2},{7,3},{8,12},{9,13},{10,... | collective-permute-start | bytes 393224 | tf_op jit(solution)/shard_map/ppermute | solution.py:35
  11.5 5.3 %collective-permute-start.2 = (bf16[2,2,32,4,256]{4,2,3,0,1:T(8,128)(2,1)S(1)}, bf16[2,2,32,4,256]{4,2,3,0,1:T(8,128)(2,1)S(1)}, u32[]{:S(2)}, u32[]{:S(2)}) collective-permute-start(bf16[2,2,32,4,256]{4,2,3,0,1:T(8,128)(2,1)S(1)} %pad_maximum_fusion.8), channel_id=1, source_target_pairs={{0,2},{1,3},{2,0},{3,1},{4,6},{5,7},{6,4},{7,5},{8,10},{9,11},{10,... | collective-permute-start | bytes 786440 | tf_op jit(solution)/shard_map/ppermute | solution.py:35
  16.9 28.6 %collective-permute-start.3 = (bf16[2,2,2,32,4,256]{5,3,4,0,1,2:T(8,128)(2,1)S(1)}, bf16[2,2,2,32,4,256]{5,3,4,0,1,2:T(8,128)(2,1)S(1)}, u32[]{:S(2)}, u32[]{:S(2)}) collective-permute-start(bf16[2,2,2,32,4,256]{5,3,4,0,1,2:T(8,128)(2,1)S(1)} %pad_maximum_fusion.6), channel_id=1, source_target_pairs={{0,1},{1,0},{2,3},{3,2},{4,5},{5,4},{6,7},{7,6},{8,9},{9,8},{10,11... | collective-permute-start | bytes 1572872 | tf_op jit(solution)/shard_map/ppermute | solution.py:35
  64.0 0.7 copy-start.1
  112.8 31.8 %copy-start = (f32[32,4,256]{2,1,0:T(4,128)S(1)}, f32[32,4,256]{2,1,0:T(4,128)}, u32[]{:S(2)}) copy-start(f32[32,4,256]{2,1,0:T(4,128)} %param.11) | copy-start | bytes 393220
  112.8 36.3 %copy-start.4 = (s32[4,2]{0,1:T(2,128)S(1)}, s32[4,2]{0,1:T(2,128)}, u32[]{:S(2)}) copy-start(s32[4,2]{0,1:T(2,128)} %param.10) | copy-start | bytes 100
  144.6 4.5 %collective-permute-start.4 = (f32[1,4,256]{2,0,1:T(1,128)S(1)}, f32[1,4,256]{2,0,1:T(1,128)S(1)}, u32[]{:S(2)}, u32[]{:S(2)}) collective-permute-start(f32[1,4,256]{2,0,1:T(1,128)S(1)} %get-tuple-element.39), channel_id=1, source_target_pairs={{0,1},{1,2},{2,3},{3,4},{4,5},{5,6},{6,7},{7,8},{8,9},{9,10},{10,1... | collective-permute-start | bytes 12296 | tf_op jit(solution)/shard_map/ppermute | solution.py:19
  147.2 4.9 %collective-permute-start.5 = (f32[1,4,256]{2,0,1:T(1,128)S(1)}, f32[1,4,256]{2,0,1:T(1,128)S(1)}, u32[]{:S(2)}, u32[]{:S(2)}) collective-permute-start(f32[1,4,256]{2,0,1:T(1,128)S(1)} %get-tuple-element.40), channel_id=1, source_target_pairs={{1,0},{2,1},{3,2},{4,3},{5,4},{6,5},{7,6},{8,7},{9,8},{10,9},{11,1... | collective-permute-start | bytes 12296 | tf_op jit(solution)/shard_map/ppermute | solution.py:21
  152.3 4.4 %collective-permute-start.6 = (f32[2,4,256]{2,0,1:T(2,128)S(1)}, f32[2,4,256]{2,0,1:T(2,128)S(1)}, u32[]{:S(2)}, u32[]{:S(2)}) collective-permute-start(f32[2,4,256]{2,0,1:T(2,128)S(1)} %get-tuple-element.37), channel_id=1, source_target_pairs={{0,1},{1,2},{2,3},{3,4},{4,5},{5,6},{6,7},{7,8},{8,9},{9,10},{10,1... | collective-permute-start | bytes 24584 | tf_op jit(solution)/shard_map/ppermute | solution.py:19
  154.3 6.4 %collective-permute-start.7 = (f32[2,4,256]{2,0,1:T(2,128)S(1)}, f32[2,4,256]{2,0,1:T(2,128)S(1)}, u32[]{:S(2)}, u32[]{:S(2)}) collective-permute-start(f32[2,4,256]{2,0,1:T(2,128)S(1)} %get-tuple-element.38), channel_id=1, source_target_pairs={{1,0},{2,1},{3,2},{4,3},{5,4},{6,5},{7,6},{8,7},{9,8},{10,9},{11,1... | collective-permute-start | bytes 24584 | tf_op jit(solution)/shard_map/ppermute | solution.py:21
  156.7 20.8 %copy-start.2 = (f32[4]{0:T(128)}, f32[4]{0:T(128)S(1)}, u32[]{:S(2)}) copy-start(f32[4]{0:T(128)S(1)} %get-tuple-element.46) | copy-start | bytes 52
  160.9 4.9 %collective-permute-start.8 = (bf16[32,4,256]{2,0,1:T(8,128)(2,1)S(1)}, bf16[32,4,256]{2,0,1:T(8,128)(2,1)S(1)}, u32[]{:S(2)}, u32[]{:S(2)}) collective-permute-start(bf16[32,4,256]{2,0,1:T(8,128)(2,1)S(1)} %get-tuple-element.7), channel_id=1, source_target_pairs={{0,8},{1,9},{2,10},{3,11},{4,12},{5,13},{6,14},{7,15},{8,0},{9,1},... | collective-permute-start | bytes 196616 | tf_op jit(solution)/shard_map/ppermute | solution.py:35
  165.8 3.9 %collective-permute-start.9 = (bf16[2,32,4,256]{3,1,2,0:T(8,128)(2,1)S(1)}, bf16[2,32,4,256]{3,1,2,0:T(8,128)(2,1)S(1)}, u32[]{:S(2)}, u32[]{:S(2)}) collective-permute-start(bf16[2,32,4,256]{3,1,2,0:T(8,128)(2,1)S(1)} %pad_maximum_fusion.22), channel_id=1, source_target_pairs={{0,4},{1,5},{2,6},{3,7},{4,0},{5,1},{6,2},{7,3},{8,12},{9,13},{10,... | collective-permute-start | bytes 393224 | tf_op jit(solution)/shard_map/ppermute | solution.py:35
  169.7 7.6 %collective-permute-start.10 = (bf16[2,2,32,4,256]{4,2,3,0,1:T(8,128)(2,1)S(1)}, bf16[2,2,32,4,256]{4,2,3,0,1:T(8,128)(2,1)S(1)}, u32[]{:S(2)}, u32[]{:S(2)}) collective-permute-start(bf16[2,2,32,4,256]{4,2,3,0,1:T(8,128)(2,1)S(1)} %pad_maximum_fusion.10), channel_id=1, source_target_pairs={{0,2},{1,3},{2,0},{3,1},{4,6},{5,7},{6,4},{7,5},{8,10},{9,11},{10,... | collective-permute-start | bytes 786440 | tf_op jit(solution)/shard_map/ppermute | solution.py:35
  177.4 3.7 %collective-permute-start.11 = (bf16[2,2,2,32,4,256]{5,3,4,0,1,2:T(8,128)(2,1)S(1)}, bf16[2,2,2,32,4,256]{5,3,4,0,1,2:T(8,128)(2,1)S(1)}, u32[]{:S(2)}, u32[]{:S(2)}) collective-permute-start(bf16[2,2,2,32,4,256]{5,3,4,0,1,2:T(8,128)(2,1)S(1)} %pad_maximum_fusion.7), channel_id=1, source_target_pairs={{0,1},{1,0},{2,3},{3,2},{4,5},{5,4},{6,7},{7,6},{8,9},{9,8},{10,11... | collective-permute-start | bytes 1572872 | tf_op jit(solution)/shard_map/ppermute | solution.py:35
  238.4 46.3 %copy-start.3 = (f32[4]{0:T(128)S(1)}, f32[4]{0:T(128)}, u32[]{:S(2)}) copy-start(f32[4]{0:T(128)} %copy-done.2) | copy-start | bytes 52
  268.7 4.5 %collective-permute-start.12 = (f32[1,4,256]{2,0,1:T(1,128)S(1)}, f32[1,4,256]{2,0,1:T(1,128)S(1)}, u32[]{:S(2)}, u32[]{:S(2)}) collective-permute-start(f32[1,4,256]{2,0,1:T(1,128)S(1)} %get-tuple-element.33), channel_id=1, source_target_pairs={{0,1},{1,2},{2,3},{3,4},{4,5},{5,6},{6,7},{7,8},{8,9},{9,10},{10,1... | collective-permute-start | bytes 12296 | tf_op jit(solution)/shard_map/ppermute | solution.py:19
  271.2 4.9 %collective-permute-start.13 = (f32[1,4,256]{2,0,1:T(1,128)S(1)}, f32[1,4,256]{2,0,1:T(1,128)S(1)}, u32[]{:S(2)}, u32[]{:S(2)}) collective-permute-start(f32[1,4,256]{2,0,1:T(1,128)S(1)} %get-tuple-element.34), channel_id=1, source_target_pairs={{1,0},{2,1},{3,2},{4,3},{5,4},{6,5},{7,6},{8,7},{9,8},{10,9},{11,1... | collective-permute-start | bytes 12296 | tf_op jit(solution)/shard_map/ppermute | solution.py:21
  276.3 4.3 %collective-permute-start.14 = (f32[2,4,256]{2,0,1:T(2,128)S(1)}, f32[2,4,256]{2,0,1:T(2,128)S(1)}, u32[]{:S(2)}, u32[]{:S(2)}) collective-permute-start(f32[2,4,256]{2,0,1:T(2,128)S(1)} %get-tuple-element.31), channel_id=1, source_target_pairs={{0,1},{1,2},{2,3},{3,4},{4,5},{5,6},{6,7},{7,8},{8,9},{9,10},{10,1... | collective-permute-start | bytes 24584 | tf_op jit(solution)/shard_map/ppermute | solution.py:19
  278.3 6.4 %collective-permute-start.15 = (f32[2,4,256]{2,0,1:T(2,128)S(1)}, f32[2,4,256]{2,0,1:T(2,128)S(1)}, u32[]{:S(2)}, u32[]{:S(2)}) collective-permute-start(f32[2,4,256]{2,0,1:T(2,128)S(1)} %get-tuple-element.32), channel_id=1, source_target_pairs={{1,0},{2,1},{3,2},{4,3},{5,4},{6,5},{7,6},{8,7},{9,8},{10,9},{11,1... | collective-permute-start | bytes 24584 | tf_op jit(solution)/shard_map/ppermute | solution.py:21
where the time goes:
time: 288 us; the launch traced here: 286 us
  matrix products  89.6 us (31%)
  blocking collectives  61.6 us (21%)
  starting transfers between devices  35.5 us (12%)
  waiting for transfers between devices  34.6 us (12%)
  local copies, waits for them, and re-layouts  31.9 us (11%)
  other arithmetic  31.8 us (11%)
    all_to_all x2, blocking collectives, sum_rows(): lax.all_to_all(chunks.astype(jnp.bfloat16), axis, 0, 0, tiled=True)  61.6 us
    dot_general x2, matrix products, block_gradient(): summed = jnp.einsum('cs,kczl->kszl', mix_block, weighted)  47.6 us
    ppermute x8, waiting for transfers between devices, gather_rows(): lax.ppermute(joined, axis, [(i, i ^ 1 << bit) for i in range(count)])  20.7 us
    ppermute x8, starting transfers between devices, gather_rows(): lax.ppermute(joined, axis, [(i, i ^ 1 << bit) for i in range(count)])  18 us
    convert_element_type x2, local copies, waits for them, and re-layouts, block_gradient(): return summed.astype(jnp.bfloat16)  15.8 us
    ppermute x4, waiting for transfers between devices, padded_2(): lax.ppermute(head, axis, [((i + 1) % count, i) for i in range(ends)])  13.9 us
    mul x1, other arithmetic, block_gradient(): weighted = weight[None, :, None, None] * beam_gain * residual  11.7 us
    convert_element_type x1, other arithmetic, block_gradient(): beam_gain = beam_block.astype(jnp.float32)[:, :, None, :]  11.3 us
  transfers between devices with their start and end apart: 16, of which 11 were waited for; matrix products, arithmetic and copies ran while one was open for 9% of the time, Pallas kernels for 0%

commit v1 on v0

--- a/solution.py
+++ b/solution.py
@@ -23,6 +23,13 @@
             axis=dim,
         )
     return cells
+
+
+def gather_all(strip, axis):
+    count = lax.axis_size(axis)
+    copies = jnp.broadcast_to(strip[None], (count,) + strip.shape)
+    joined = lax.all_to_all(copies, axis, 0, 0, tiled=True)
+    return joined.reshape((count * strip.shape[0],) + strip.shape[1:])
 
 
 def gather_rows(strip, axis):
@@ -140,10 +147,12 @@
     bounds = threshold_levels.astype(jnp.float32) * 0.05
     fine_bound = bounds[:, 0][:, None]
     coarse_bound = bounds[:, 1][:, None]
+    first_row = lax.axis_index("chan") * strip_rows
     sources = start_sources
     for iteration in range(ITERS):
         rounded = sources.astype(jnp.bfloat16)
-        gathered = gather_rows(rounded, "chan")
+        gather = gather_all if iteration == 0 else gather_rows
+        gathered = gather(rounded, "chan")
         packed = column_part(gathered, col_cat)
         fourier = combine_forward(
             jnp.dot(row_real, packed, preferred_element_type=jnp.float32),
@@ -158,10 +167,14 @@
             "chan",
         )
         updated = sources + gradient
-        fine_pad = padded_2(updated, (("chan", 0),), 1)
-        smooth_one = smooth_cols(smooth_rows(fine_pad, 1, strip_rows), 1)
-        coarse_pad = padded_2(smooth_one, (("chan", 0),), 2)
-        coarse = smooth_cols(smooth_rows(coarse_pad, 2, strip_rows), 2)
+        wide_pad = padded_2(updated, (("chan", 0),), 3)
+        smooth_wide = smooth_cols(smooth_rows(wide_pad, 1, strip_rows + 4), 1)
+        inside = (first_row - 2 + jnp.arange(strip_rows + 4) >= 0) & (
+            first_row - 2 + jnp.arange(strip_rows + 4) < full_rows
+        )
+        smooth_wide = jnp.where(inside[:, None, None], smooth_wide, 0.0)
+        smooth_one = smooth_wide[2 : 2 + strip_rows]
+        coarse = smooth_cols(smooth_rows(smooth_wide, 2, strip_rows), 2)
         sources = combine_scales(updated, smooth_one, coarse, fine_bound, coarse_bound)
     return sources
 

time: 288 us -> 265 us (0.920)
  blocking collectives: 61.6 us -> 30.9 us
  waiting for transfers between devices: 34.6 us -> 40.1 us
    all_to_all x2 -> x1, blocking collectives: 61.6 us -> 30.9 us  [sum_rows(): lax.all_to_all(chunks.astype(jnp.bfloat16), axis, 0, 0, tiled=True)]
    all_to_all x0 -> x2, waiting for transfers between devices: none -> 23.1 us  [the longest x1 23.1 us: sum_rows(): lax.all_to_all(chunks.astype(jnp.bfloat16), axis, 0, 0, tiled=True)]
    all_to_all x0 -> x2, starting transfers between devices: none -> 13.5 us  [the longest x1 7.35 us: gather_all(): joined = lax.all_to_all(copies, axis, 0, 0, tiled=True)]
    ppermute x8 -> x4, waiting for transfers between devices: 20.7 us -> 10.8 us  [gather_rows(): lax.ppermute(joined, axis, [(i, i ^ 1 << bit) for i in range(count)])]
    ppermute x4 -> x2, waiting for transfers between devices: 13.9 us -> 6.21 us  [padded_2(): lax.ppermute(head, axis, [((i + 1) % count, i) for i in range(ends)])]
    ppermute x8 -> x4, starting transfers between devices: 18 us -> 10.7 us  [gather_rows(): lax.ppermute(joined, axis, [(i, i ^ 1 << bit) for i in range(count)])]
    ppermute x4 -> x2, starting transfers between devices: 8.59 us -> 3.84 us  [padded_2(): lax.ppermute(head, axis, [((i + 1) % count, i) for i in range(ends)])]
    ppermute x4 -> x2, starting transfers between devices: 8.94 us -> 5.74 us  [padded_2(): lax.ppermute(tail, axis, [(i, (i + 1) % count) for i in range(ends)])]
  transfers between devices with their start and end apart: 16 -> 10, of which waited for: 11 -> 7; matrix products, arithmetic and copies ran while one was open for 9% -> 9% of each run, Pallas kernels for 0% -> 0%
where the time goes in v1:
time: 265 us; the launch traced here: 263 us
  matrix products  92.3 us (35%)
  waiting for transfers between devices  40.1 us (15%)
  local copies, waits for them, and re-layouts  34.2 us (13%)
  starting transfers between devices  33.8 us (13%)
  other arithmetic  30.9 us (12%)
  blocking collectives  30.9 us (12%)
    dot_general x2, matrix products, block_gradient(): summed = jnp.einsum('cs,kczl->kszl', mix_block, weighted)  47.6 us
    all_to_all x1, blocking collectives, sum_rows(): lax.all_to_all(chunks.astype(jnp.bfloat16), axis, 0, 0, tiled=True)  30.9 us
    all_to_all x1, waiting for transfers between devices, sum_rows(): lax.all_to_all(chunks.astype(jnp.bfloat16), axis, 0, 0, tiled=True)  23.1 us
    convert_element_type x2, local copies, waits for them, and re-layouts, block_gradient(): return summed.astype(jnp.bfloat16)  15.8 us
    mul x1, other arithmetic, block_gradient(): weighted = weight[None, :, None, None] * beam_gain * residual  11.7 us
    dot_general x2, matrix products, body(): jnp.dot(row_imag, packed, preferred_element_type=jnp.float32)  11.6 us
    convert_element_type x1, other arithmetic, block_gradient(): beam_gain = beam_block.astype(jnp.float32)[:, :, None, :]  11.3 us
    ppermute x4, waiting for transfers between devices, gather_rows(): lax.ppermute(joined, axis, [(i, i ^ 1 << bit) for i in range(count)])  10.8 us
  transfers between devices with their start and end apart: 10, of which 7 were waited for; matrix products, arithmetic and copies ran while one was open for 9% of the time, Pallas kernels for 0%

profile of v1, /device:TPU:1, one launch (start us, length us, event | category | flops | bytes accessed | tf_op | source)
XLA Modules:
  0.0 262.8 jit_solution(6368787715641451263)
XLA Ops:
  2.3 7.3 %all-to-all-start = ((bf16[16,32,4,256]{3,2,1,0:T(4,128)(2,1)}), bf16[16,32,4,256]{3,2,1,0:T(4,128)(2,1)S(1)}, u32[]{:S(2)}, u32[]{:S(2)}) async-start(bf16[16,32,4,256]{3,2,1,0:T(4,128)(2,1)} %broadcast_in_dim.43), calls=%async_computation | async-start | bytes 2097152 | tf_op jit(solution)/shard_map/all_to_all | solution.py:31
  9.7 11.3 %convert_element_type.123 = f32[512,32,256]{2,1,0:T(8,128)} convert(bf16[512,32,256]{2,1,0:T(8,128)(2,1)} %param.7) | non-fusion elementwise | flops 4194304 | bytes 25165824 | tf_op jit(solution)/shard_map/convert_element_type | solution.py:103
  22.1 11.7 %broadcast_multiply_fusion = f32[512,32,256]{2,1,0:T(8,128)} fusion(f32[32]{0:T(128)S(1)} %convert_multiply_fusion.1, bf16[512,32,256]{2,1,0:T(8,128)(2,1)} %param.7), kind=kLoop, calls=%fused_computation.16 | loop fusion | flops 8388608 | bytes 25165952 | tf_op jit(solution)/shard_map/mul | solution.py:106
  37.4 3.1 %reshape.78 = bf16[512,2048]{1,0:T(8,128)(2,1)S(1)} reshape(bf16[2048,512]{1,0:T(8,128)(2,1)} %copy.28) | data formatting | bytes 4194304 | tf_op jit(solution)/shard_map/reshape | solution.py:76
  43.3 6.6 %fusion.63 = f32[512,4,2,256]{3,0,2,1:T(8,128)S(1)} fusion(bf16[4,2,256,512]{3,2,1,0:T(8,128)(2,1)} %bitcast.109), kind=kOutput, calls=%fused_computation.74 | convolution fusion | flops 1078198272 | bytes 6291456 | tf_op jit(solution)/shard_map/dot_general | solution.py:159
  50.0 4.9 %fusion.69 = f32[512,4,2,256]{3,0,2,1:T(8,128)S(1)} fusion(bf16[4,2,256,512]{3,2,1,0:T(8,128)(2,1)S(1)} %bitcast.110), kind=kOutput, calls=%fused_computation.76 | convolution fusion | flops 1077936128 | bytes 6291456 | tf_op jit(solution)/shard_map/dot_general | solution.py:158
  56.5 23.7 %convert_bitcast_fusion.1 = bf16[512,4,2,256]{3,1,2,0:T(4,128)(2,1)} fusion(f32[512,32,256]{2,1,0:T(8,128)} %convert_element_type.123, f32[512,32,256]{2,1,0:T(8,128)} %broadcast_multiply_fusion, bf16[512,32,2,256]{3,2,1,0:T(2,128)(2,1)} %param.6, bf16[512,4,2,256]{3,0,2,1:T(8,128)(2,1)S(1)} %pad_maximum_fusion, f32[32,4]{0,1:T(4,128)S(1)} %copy-done.2), kind=kOutput, calls=%fused_computation.53 | convolution fusion | flops 176160896 | bytes 54526464 | tf_op jit(solution)/shard_map/cs,kczl->kszl/dot_general | solution.py:107
  80.2 12.8 %copy.32 = bf16[512,4,2,256]{0,3,2,1:T(8,128)(2,1)S(1)} copy(bf16[512,4,2,256]{3,1,2,0:T(4,128)(2,1)} %convert_bitcast_fusion.1) | data formatting | bytes 4194304 | tf_op jit(solution)/shard_map/convert_element_type | solution.py:108
  93.0 4.9 %fusion.33 = f32[512,4,2,256]{3,0,2,1:T(8,128)S(1)} fusion(bf16[512,4,2,256]{0,3,2,1:T(8,128)(2,1)S(1)} %copy.32), kind=kOutput, calls=%fused_computation.46 | convolution fusion | flops 1078198272 | bytes 6291456 | tf_op jit(solution)/shard_map/dot_general | solution.py:89
  97.9 4.9 %fusion.35 = f32[512,4,2,256]{3,0,2,1:T(8,128)S(1)} fusion(bf16[512,4,2,256]{0,3,2,1:T(8,128)(2,1)S(1)} %copy.32), kind=kOutput, calls=%fused_computation.48 | convolution fusion | flops 1077936128 | bytes 6291456 | tf_op jit(solution)/shard_map/dot_general | solution.py:88
  105.5 6.1 %all-to-all-start.1 = ((bf16[16,32,4,256]{3,1,2,0:T(8,128)(2,1)}), bf16[16,32,4,256]{3,1,2,0:T(8,128)(2,1)S(1)}, u32[]{:S(2)}, u32[]{:S(2)}) async-start(bf16[16,32,4,256]{3,1,2,0:T(8,128)(2,1)} %fusion.45), calls=%async_computation.1 | async-start | bytes 2097152 | tf_op jit(solution)/shard_map/all_to_all | solution.py:53
  111.7 23.1 %all-to-all-done.1 = bf16[16,32,4,256]{3,1,2,0:T(8,128)(2,1)S(1)} async-done(((bf16[16,32,4,256]{3,1,2,0:T(8,128)(2,1)}), bf16[16,32,4,256]{3,1,2,0:T(8,128)(2,1)S(1)}, u32[]{:S(2)}, u32[]{:S(2)}) %all-to-all-start.1) | async-done | bytes 1048608 | tf_op jit(solution)/shard_map/all_to_all | solution.py:53
  135.0 3.2 %collective-permute-start = (f32[3,4,256]{2,0,1:T(4,128)S(1)}, f32[3,4,256]{2,0,1:T(4,128)S(1)}, u32[]{:S(2)}, u32[]{:S(2)}) collective-permute-start(f32[3,4,256]{2,0,1:T(4,128)S(1)} %get-tuple-element.25), channel_id=1, source_target_pairs={{0,1},{1,2},{2,3},{3,4},{4,5},{5,6},{6,7},{7,8},{8,9},{9,10},{10,1... | collective-permute-start | bytes 36872 | tf_op jit(solution)/shard_map/ppermute | solution.py:19
  140.2 3.1 %collective-permute-done.1 = f32[3,4,256]{2,0,1:T(4,128)S(1)} collective-permute-done((f32[3,4,256]{2,0,1:T(4,128)S(1)}, f32[3,4,256]{2,0,1:T(4,128)S(1)}, u32[]{:S(2)}, u32[]{:S(2)}) %collective-permute-start.1) | collective-permute-done | bytes 12320 | tf_op jit(solution)/shard_map/ppermute | solution.py:21
  148.2 3.5 %collective-permute-start.3 = (bf16[2,32,4,256]{3,1,2,0:T(8,128)(2,1)S(1)}, bf16[2,32,4,256]{3,1,2,0:T(8,128)(2,1)S(1)}, u32[]{:S(2)}, u32[]{:S(2)}) collective-permute-start(bf16[2,32,4,256]{3,1,2,0:T(8,128)(2,1)S(1)} %pad_maximum_fusion.12), channel_id=1, source_target_pairs={{0,4},{1,5},{2,6},{3,7},{4,0},{5,1},{6,2},{7,3},{8,12},{9,13},{10,... | collective-permute-start | bytes 393224 | tf_op jit(solution)/shard_map/ppermute | solution.py:42
  156.5 5.2 %collective-permute-done.4 = bf16[2,2,32,4,256]{4,2,3,0,1:T(8,128)(2,1)S(1)} collective-permute-done((bf16[2,2,32,4,256]{4,2,3,0,1:T(8,128)(2,1)S(1)}, bf16[2,2,32,4,256]{4,2,3,0,1:T(8,128)(2,1)S(1)}, u32[]{:S(2)}, u32[]{:S(2)}) %collective-permute-start.4) | collective-permute-done | bytes 262176 | tf_op jit(solution)/shard_map/ppermute | solution.py:42
  173.4 4.9 %fusion.60 = f32[512,4,2,256]{3,0,2,1:T(8,128)S(1)} fusion(bf16[4,2,256,512]{3,2,1,0:T(8,128)(2,1)S(1)} %bitcast.111), kind=kOutput, calls=%fused_computation.73 | convolution fusion | flops 1078198272 | bytes 6291456 | tf_op jit(solution)/shard_map/dot_general | solution.py:159
  178.3 4.9 %fusion.66 = f32[512,4,2,256]{3,0,2,1:T(8,128)S(1)} fusion(bf16[4,2,256,512]{3,2,1,0:T(8,128)(2,1)S(1)} %bitcast.112), kind=kOutput, calls=%fused_computation.75 | convolution fusion | flops 1077936128 | bytes 6291456 | tf_op jit(solution)/shard_map/dot_general | solution.py:158
  184.3 23.9 %convert_bitcast_fusion = bf16[512,4,2,256]{3,1,2,0:T(4,128)(2,1)} fusion(f32[512,32,256]{2,1,0:T(8,128)} %convert_element_type.123, f32[512,32,256]{2,1,0:T(8,128)} %broadcast_multiply_fusion, bf16[512,32,2,256]{3,2,1,0:T(2,128)(2,1)} %param.6, bf16[512,4,2,256]{3,0,2,1:T(8,128)(2,1)S(1)} %pad_maximum_fusion.1, f32[32,4]{0,1:T(4,128)S(1)} %copy-done.2), kind=kOutput, calls=%fused_computation.51 | convolution fusion | flops 176160896 | bytes 54526464 | tf_op jit(solution)/shard_map/cs,kczl->kszl/dot_general | solution.py:107
  208.2 3.0 %copy.39 = bf16[512,4,2,256]{0,3,2,1:T(8,128)(2,1)S(1)} copy(bf16[512,4,2,256]{3,1,2,0:T(4,128)(2,1)} %convert_bitcast_fusion) | data formatting | bytes 4194304 | tf_op jit(solution)/shard_map/convert_element_type | solution.py:108
  211.2 4.9 %fusion.27 = f32[512,4,2,256]{3,0,2,1:T(8,128)S(1)} fusion(bf16[512,4,2,256]{0,3,2,1:T(8,128)(2,1)S(1)} %copy.39), kind=kOutput, calls=%fused_computation.40 | convolution fusion | flops 1078198272 | bytes 6291456 | tf_op jit(solution)/shard_map/dot_general | solution.py:89
  216.1 4.9 %fusion.29 = f32[512,4,2,256]{3,0,2,1:T(8,128)S(1)} fusion(bf16[512,4,2,256]{0,3,2,1:T(8,128)(2,1)S(1)} %copy.39), kind=kOutput, calls=%fused_computation.42 | convolution fusion | flops 1077936128 | bytes 6291456 | tf_op jit(solution)/shard_map/dot_general | solution.py:88
  222.7 30.9 %all_to_all.15 = bf16[16,32,4,256]{3,1,2,0:T(8,128)(2,1)S(1)} all-to-all(bf16[16,32,4,256]{3,1,2,0:T(8,128)(2,1)S(1)} %fusion.48), channel_id=1, replica_groups=mesh['groups'=2,'chan'=16] {'chan'}, dimensions={0} | all-to-all | bytes 2097152 | tf_op jit(solution)/shard_map/all_to_all | solution.py:53
  258.3 3.1 %collective-permute-done.7 = f32[3,4,256]{2,0,1:T(4,128)S(1)} collective-permute-done((f32[3,4,256]{2,0,1:T(4,128)S(1)}, f32[3,4,256]{2,0,1:T(4,128)S(1)}, u32[]{:S(2)}, u32[]{:S(2)}) %collective-permute-start.7) | collective-permute-done | bytes 12320 | tf_op jit(solution)/shard_map/ppermute | solution.py:21
  (79 shorter events, 46.2 us)
Async XLA Ops:
  2.3 31.5 %all-to-all-start = ((bf16[16,32,4,256]{3,2,1,0:T(4,128)(2,1)}), bf16[16,32,4,256]{3,2,1,0:T(4,128)(2,1)S(1)}, u32[]{:S(2)}, u32[]{:S(2)}) async-start(bf16[16,32,4,256]{3,2,1,0:T(4,128)(2,1)} %broadcast_in_dim.43), calls=%async_computation | async-start | bytes 2097152 | tf_op jit(solution)/shard_map/all_to_all | solution.py:31
  9.7 12.4 %copy-start.8 = (s32[32]{0:T(128)S(1)}, s32[32]{0:T(128)}, u32[]{:S(2)}) copy-start(s32[32]{0:T(128)} %param.9) | copy-start | bytes 388
  43.3 6.7 %copy-start = (bf16[2048,512]{1,0:T(8,128)(2,1)S(1)}, bf16[2048,512]{1,0:T(8,128)(2,1)}, u32[]{:S(2)}) copy-start(bf16[2048,512]{1,0:T(8,128)(2,1)} %copy.49) | copy-start | bytes 6291460
  55.8 0.7 copy-start.2
  105.5 6.2 %copy-start.7 = (s32[4,2]{0,1:T(2,128)S(1)}, s32[4,2]{0,1:T(2,128)}, u32[]{:S(2)}) copy-start(s32[4,2]{0,1:T(2,128)} %param.10) | copy-start | bytes 100
  105.5 29.5 %copy-start.1 = (f32[32,4,256]{2,1,0:T(4,128)S(1)}, f32[32,4,256]{2,1,0:T(4,128)}, u32[]{:S(2)}) copy-start(f32[32,4,256]{2,1,0:T(4,128)} %param.11) | copy-start | bytes 393220
  105.5 29.3 %all-to-all-start.1 = ((bf16[16,32,4,256]{3,1,2,0:T(8,128)(2,1)}), bf16[16,32,4,256]{3,1,2,0:T(8,128)(2,1)S(1)}, u32[]{:S(2)}, u32[]{:S(2)}) async-start(bf16[16,32,4,256]{3,1,2,0:T(8,128)(2,1)} %fusion.45), calls=%async_computation.1 | async-start | bytes 2097152 | tf_op jit(solution)/shard_map/all_to_all | solution.py:53
  111.7 32.1 %copy-start.3 = (f32[4]{0:T(128)}, f32[4]{0:T(128)S(1)}, u32[]{:S(2)}) copy-start(f32[4]{0:T(128)S(1)} %get-tuple-element.30) | copy-start | bytes 52
  135.0 5.2 %collective-permute-start = (f32[3,4,256]{2,0,1:T(4,128)S(1)}, f32[3,4,256]{2,0,1:T(4,128)S(1)}, u32[]{:S(2)}, u32[]{:S(2)}) collective-permute-start(f32[3,4,256]{2,0,1:T(4,128)S(1)} %get-tuple-element.25), channel_id=1, source_target_pairs={{0,1},{1,2},{2,3},{3,4},{4,5},{5,6},{6,7},{7,8},{8,9},{9,10},{10,1... | collective-permute-start | bytes 36872 | tf_op jit(solution)/shard_map/ppermute | solution.py:19
  138.3 5.1 %collective-permute-start.1 = (f32[3,4,256]{2,0,1:T(4,128)S(1)}, f32[3,4,256]{2,0,1:T(4,128)S(1)}, u32[]{:S(2)}, u32[]{:S(2)}) collective-permute-start(f32[3,4,256]{2,0,1:T(4,128)S(1)} %get-tuple-element.26), channel_id=1, source_target_pairs={{1,0},{2,1},{3,2},{4,3},{5,4},{6,5},{7,6},{8,7},{9,8},{10,9},{11,1... | collective-permute-start | bytes 36872 | tf_op jit(solution)/shard_map/ppermute | solution.py:21
  140.2 3.4 %copy-start.5 = (pred[36]{0:T(512)(128)(4,1)}, pred[36]{0:T(512)(128)(4,1)S(1)}, u32[]{:S(2)}) copy-start(pred[36]{0:T(512)(128)(4,1)S(1)} %compare_and_fusion) | copy-start | bytes 112
  143.8 4.4 %collective-permute-start.2 = (bf16[32,4,256]{2,0,1:T(8,128)(2,1)S(1)}, bf16[32,4,256]{2,0,1:T(8,128)(2,1)S(1)}, u32[]{:S(2)}, u32[]{:S(2)}) collective-permute-start(bf16[32,4,256]{2,0,1:T(8,128)(2,1)S(1)} %get-tuple-element.5), channel_id=1, source_target_pairs={{0,8},{1,9},{2,10},{3,11},{4,12},{5,13},{6,14},{7,15},{8,0},{9,1},... | collective-permute-start | bytes 196616 | tf_op jit(solution)/shard_map/ppermute | solution.py:42
  148.2 5.9 %collective-permute-start.3 = (bf16[2,32,4,256]{3,1,2,0:T(8,128)(2,1)S(1)}, bf16[2,32,4,256]{3,1,2,0:T(8,128)(2,1)S(1)}, u32[]{:S(2)}, u32[]{:S(2)}) collective-permute-start(bf16[2,32,4,256]{3,1,2,0:T(8,128)(2,1)S(1)} %pad_maximum_fusion.12), channel_id=1, source_target_pairs={{0,4},{1,5},{2,6},{3,7},{4,0},{5,1},{6,2},{7,3},{8,12},{9,13},{10,... | collective-permute-start | bytes 393224 | tf_op jit(solution)/shard_map/ppermute | solution.py:42
  154.2 7.4 %collective-permute-start.4 = (bf16[2,2,32,4,256]{4,2,3,0,1:T(8,128)(2,1)S(1)}, bf16[2,2,32,4,256]{4,2,3,0,1:T(8,128)(2,1)S(1)}, u32[]{:S(2)}, u32[]{:S(2)}) collective-permute-start(bf16[2,2,32,4,256]{4,2,3,0,1:T(8,128)(2,1)S(1)} %pad_maximum_fusion.7), channel_id=1, source_target_pairs={{0,2},{1,3},{2,0},{3,1},{4,6},{5,7},{6,4},{7,5},{8,10},{9,11},{10,... | collective-permute-start | bytes 786440 | tf_op jit(solution)/shard_map/ppermute | solution.py:42
  161.8 3.7 %collective-permute-start.5 = (bf16[2,2,2,32,4,256]{5,3,4,0,1,2:T(8,128)(2,1)S(1)}, bf16[2,2,2,32,4,256]{5,3,4,0,1,2:T(8,128)(2,1)S(1)}, u32[]{:S(2)}, u32[]{:S(2)}) collective-permute-start(bf16[2,2,2,32,4,256]{5,3,4,0,1,2:T(8,128)(2,1)S(1)} %pad_maximum_fusion.5), channel_id=1, source_target_pairs={{0,1},{1,0},{2,3},{3,2},{4,5},{5,4},{6,7},{7,6},{8,9},{9,8},{10,11... | collective-permute-start | bytes 1572872 | tf_op jit(solution)/shard_map/ppermute | solution.py:42
  222.7 38.8 %copy-start.6 = (pred[36]{0:T(512)(128)(4,1)S(1)}, pred[36]{0:T(512)(128)(4,1)}, u32[]{:S(2)}) copy-start(pred[36]{0:T(512)(128)(4,1)} %copy-done.5) | copy-start | bytes 112
  253.6 8.1 %copy-start.4 = (f32[4]{0:T(128)S(1)}, f32[4]{0:T(128)}, u32[]{:S(2)}) copy-start(f32[4]{0:T(128)} %copy-done.3) | copy-start | bytes 52
  253.8 4.5 %collective-permute-start.6 = (f32[3,4,256]{2,0,1:T(4,128)S(1)}, f32[3,4,256]{2,0,1:T(4,128)S(1)}, u32[]{:S(2)}, u32[]{:S(2)}) collective-permute-start(f32[3,4,256]{2,0,1:T(4,128)S(1)} %get-tuple-element.21), channel_id=1, source_target_pairs={{0,1},{1,2},{2,3},{3,4},{4,5},{5,6},{6,7},{7,8},{8,9},{9,10},{10,1... | collective-permute-start | bytes 36872 | tf_op jit(solution)/shard_map/ppermute | solution.py:19
  256.4 5.1 %collective-permute-start.7 = (f32[3,4,256]{2,0,1:T(4,128)S(1)}, f32[3,4,256]{2,0,1:T(4,128)S(1)}, u32[]{:S(2)}, u32[]{:S(2)}) collective-permute-start(f32[3,4,256]{2,0,1:T(4,128)S(1)} %get-tuple-element.22), channel_id=1, source_target_pairs={{1,0},{2,1},{3,2},{4,3},{5,4},{6,5},{7,6},{8,7},{9,8},{10,9},{11,1... | collective-permute-start | bytes 36872 | tf_op jit(solution)/shard_map/ppermute | solution.py:21

commit v2 on v1

--- a/solution.py
+++ b/solution.py
@@ -49,9 +49,20 @@
 
 def sum_rows(values, axis):
     count = lax.axis_size(axis)
-    chunks = values.reshape((count, values.shape[0] // count) + values.shape[1:])
-    received = lax.all_to_all(chunks.astype(jnp.bfloat16), axis, 0, 0, tiled=True)
-    return received.astype(jnp.float32).sum(axis=0)
+    bits = count.bit_length() - 1
+    assert 1 << bits == count
+    own = lax.axis_index(axis)
+    split = values.reshape((2,) * bits + (values.shape[0] // count,) + values.shape[1:])
+    for bit in range(bits):
+        dim = bits - 1 - bit
+        side = (own >> bit) & 1
+        keep = lax.dynamic_index_in_dim(split, side, axis=dim, keepdims=False)
+        send = lax.dynamic_index_in_dim(split, 1 - side, axis=dim, keepdims=False)
+        moved = lax.ppermute(
+            send.astype(jnp.bfloat16), axis, [(i, i ^ (1 << bit)) for i in range(count)]
+        )
+        split = keep + moved.astype(jnp.float32)
+    return split
 
 
 def dft_tables(length):
@@ -99,7 +110,10 @@
 
 
 def block_gradient(fourier, data_block, beam_block, mix_block, level_block):
-    predicted = jnp.einsum("ct,ktzl->kczl", mix_block, fourier)
+    predicted = sum(
+        mix_block[None, :, t, None, None] * fourier[:, t, None, :, :]
+        for t in range(mix_block.shape[1])
+    )
     beam_gain = beam_block.astype(jnp.float32)[:, :, None, :]
     residual = data_block.astype(jnp.float32) - beam_gain * predicted
     weight = level_block.astype(jnp.float32) * 0.25

time: 265 us -> 363 us (1.37)
  other arithmetic: 30.9 us -> 167 us
  blocking collectives: 30.9 us -> 0 us
  matrix products: 92.3 us -> 62.5 us
  local copies, waits for them, and re-layouts: 34.2 us -> 46.1 us
  starting transfers between devices: 33.8 us -> 43.7 us
    mul x1 -> x3, other arithmetic: 11.7 us -> 146 us  [block_gradient(): weighted = weight[None, :, None, None] * beam_gain * residual]
    all_to_all x1 -> x0, blocking collectives: 30.9 us -> none  [sum_rows(): lax.all_to_all(chunks.astype(jnp.bfloat16), axis, 0, 0, tiled=True)]
    dot_general x2, matrix products: 47.6 us -> 18.8 us  [block_gradient(): summed = jnp.einsum('cs,kczl->kszl', mix_block, weighted)]
    ppermute x0 -> x8, waiting for transfers between devices: none -> 24.3 us  [sum_rows(): lax.ppermute(send.astype(jnp.bfloat16), axis, [(i, i ^ 1 << bit) for i in...]
    all_to_all x1 -> x0, waiting for transfers between devices: 23.1 us -> none  [sum_rows(): lax.all_to_all(chunks.astype(jnp.bfloat16), axis, 0, 0, tiled=True)]
    mul x0 -> x9, local copies, waits for them, and re-layouts: none -> 22 us  [block_gradient(): mix_block[None, :, t, None, None] * fourier[:, t, None, :, :]]
    ppermute x0 -> x8, starting transfers between devices: none -> 12.3 us  [sum_rows(): lax.ppermute(send.astype(jnp.bfloat16), axis, [(i, i ^ 1 << bit) for i in...]
    convert_element_type x2, local copies, waits for them, and re-layouts: 15.8 us -> 5.93 us  [block_gradient(): return summed.astype(jnp.bfloat16)]
  transfers between devices with their start and end apart: 10 -> 17, of which waited for: 7 -> 14; matrix products, arithmetic and copies ran while one was open for 9% -> 7% of each run, Pallas kernels for 0% -> 0%
where the time goes in v2:
time: 363 us
  other arithmetic  167 us (46%)
  matrix products  62.5 us (17%)
  local copies, waits for them, and re-layouts  46.1 us (13%)
  starting transfers between devices  43.7 us (12%)
  waiting for transfers between devices  42.5 us (12%)
    mul x3, other arithmetic, block_gradient(): weighted = weight[None, :, None, None] * beam_gain * residual  146 us
    ppermute x8, waiting for transfers between devices, sum_rows(): lax.ppermute(send.astype(jnp.bfloat16), axis, [(i, i ^ 1 << bit) for i in...  24.3 us
    mul x9, local copies, waits for them, and re-layouts, block_gradient(): mix_block[None, :, t, None, None] * fourier[:, t, None, :, :]  22 us
    dot_general x2, matrix products, block_gradient(): summed = jnp.einsum('cs,kczl->kszl', mix_block, weighted)  18.8 us
    ppermute x8, starting transfers between devices, sum_rows(): lax.ppermute(send.astype(jnp.bfloat16), axis, [(i, i ^ 1 << bit) for i in...  12.3 us
    ppermute x4, waiting for transfers between devices, gather_rows(): lax.ppermute(joined, axis, [(i, i ^ 1 << bit) for i in range(count)])  12.1 us
    ppermute x2, starting transfers between devices, padded_2(): lax.ppermute(tail, axis, [(i, (i + 1) % count) for i in range(ends)])  11.9 us
    dot_general x2, matrix products, body(): jnp.dot(row_imag, packed, preferred_element_type=jnp.float32)  11.5 us
  transfers between devices with their start and end apart: 17, of which 14 were waited for; matrix products, arithmetic and copies ran while one was open for 7% of the time, Pallas kernels for 0%

profile of v2, /device:TPU:1, one launch (start us, length us, event | category | flops | bytes accessed | tf_op | source)
XLA Modules:
  0.0 363.2 jit_solution(2234573071610902220)
XLA Ops:
  2.3 7.3 %all-to-all-start = ((bf16[16,32,4,256]{3,2,1,0:T(4,128)(2,1)}), bf16[16,32,4,256]{3,2,1,0:T(4,128)(2,1)S(1)}, u32[]{:S(2)}, u32[]{:S(2)}) async-start(bf16[16,32,4,256]{3,2,1,0:T(4,128)(2,1)} %broadcast_in_dim.43), calls=%async_computation | async-start | bytes 2097152 | tf_op jit(solution)/shard_map/all_to_all | solution.py:31
  9.7 11.3 %convert_element_type.183 = f32[512,32,256]{2,1,0:T(8,128)} convert(bf16[512,32,256]{2,1,0:T(8,128)(2,1)} %param.7) | non-fusion elementwise | flops 4194304 | bytes 25165824 | tf_op jit(solution)/shard_map/convert_element_type | solution.py:117
  22.2 11.7 %broadcast_multiply_fusion = f32[512,32,256]{2,1,0:T(8,128)} fusion(f32[32]{0:T(128)S(1)} %convert_multiply_fusion.1, bf16[512,32,256]{2,1,0:T(8,128)(2,1)} %param.7), kind=kLoop, calls=%fused_computation.8 | loop fusion | flops 8388608 | bytes 25165952 | tf_op jit(solution)/shard_map/mul | solution.py:120
  37.5 3.1 reshape.90
  43.4 6.6 %fusion.55 = f32[512,4,2,256]{3,0,2,1:T(8,128)S(1)} fusion(bf16[4,2,256,512]{3,2,1,0:T(8,128)(2,1)} %bitcast.171), kind=kOutput, calls=%fused_computation.96 | convolution fusion | flops 1078198272 | bytes 6291456 | tf_op jit(solution)/shard_map/dot_general | solution.py:173
  50.0 4.9 %fusion.61 = f32[512,4,2,256]{3,0,2,1:T(8,128)S(1)} fusion(bf16[4,2,256,512]{3,2,1,0:T(8,128)(2,1)S(1)} %bitcast.172), kind=kOutput, calls=%fused_computation.98 | convolution fusion | flops 1077936128 | bytes 6291456 | tf_op jit(solution)/shard_map/dot_general | solution.py:172
  56.8 15.8 %copy.30 = f32[512,2,256]{2,1,0:T(2,128)S(1)} copy(f32[512,2,256]{2,0,1:T(8,128)S(1)} %get-tuple-element.20) | data formatting | bytes 2097152 | tf_op jit(solution)/shard_map/mul | solution.py:114
  74.3 67.4 %fusion = bf16[512,32,2,256]{3,2,1,0:T(2,128)(2,1)} fusion(bf16[512,32,2,256]{3,2,1,0:T(2,128)(2,1)} %param.6, f32[512,2,256]{2,1,0:T(2,128)S(1)} %copy.32, f32[512,2,256]{2,1,0:T(2,128)S(1)} %copy.31, f32[512,2,256]{2,1,0:T(2,128)S(1)} %copy.30, f32[512,2,256]{2,1,0:T(2,128)S(1)} %copy.29, f32[512,32,256]{2,1,0:T(8,128)} %convert_element_type.183, ...), kind=kLoop, calls=%fused_computation.2 | loop fusion | flops 100663296 | bytes 71303680 | tf_op jit(solution)/shard_map/mul | solution.py:120
  141.6 9.4 %convert_bitcast_fusion.1 = bf16[512,4,2,256]{3,1,2,0:T(4,128)(2,1)} fusion(bf16[512,32,2,256]{3,2,1,0:T(2,128)(2,1)} %fusion, f32[32,4]{0,1:T(4,128)S(1)} %copy-done.10), kind=kOutput, calls=%fused_computation.51 | convolution fusion | flops 67108864 | bytes 18874880 | tf_op jit(solution)/shard_map/cs,kczl->kszl/dot_general | solution.py:121
  154.0 4.9 %fusion.19 = f32[512,4,2,256]{3,0,2,1:T(8,128)S(1)} fusion(bf16[512,4,2,256]{0,3,2,1:T(8,128)(2,1)S(1)} %copy.34), kind=kOutput, calls=%fused_computation.46 | convolution fusion | flops 1078198272 | bytes 6291456 | tf_op jit(solution)/shard_map/dot_general | solution.py:100
  158.9 4.9 %fusion.21 = f32[512,4,2,256]{3,0,2,1:T(8,128)S(1)} fusion(bf16[512,4,2,256]{0,3,2,1:T(8,128)(2,1)S(1)} %copy.34), kind=kOutput, calls=%fused_computation.48 | convolution fusion | flops 1077936128 | bytes 6291456 | tf_op jit(solution)/shard_map/dot_general | solution.py:99
  170.4 6.4 %collective-permute-done.1 = bf16[2,2,32,4,256]{4,2,3,1,0:T(8,128)(2,1)S(1)} collective-permute-done((bf16[2,2,32,4,256]{4,2,3,1,0:T(8,128)(2,1)S(1)}, bf16[2,2,32,4,256]{4,2,3,1,0:T(8,128)(2,1)S(1)}, u32[]{:S(2)}, u32[]{:S(2)}) %collective-permute-start.1) | collective-permute-done | bytes 262176 | tf_op jit(solution)/shard_map/ppermute | solution.py:61
  186.0 5.6 %collective-permute-start.4 = (f32[3,4,256]{2,0,1:T(4,128)S(1)}, f32[3,4,256]{2,0,1:T(4,128)S(1)}, u32[]{:S(2)}, u32[]{:S(2)}) collective-permute-start(f32[3,4,256]{2,0,1:T(4,128)S(1)} %get-tuple-element.33), channel_id=1, source_target_pairs={{0,1},{1,2},{2,3},{3,4},{4,5},{5,6},{6,7},{7,8},{8,9},{9,10},{10,1... | collective-permute-start | bytes 36872 | tf_op jit(solution)/shard_map/ppermute | solution.py:19
  208.9 5.3 %collective-permute-done.8 = bf16[2,2,32,4,256]{4,2,3,0,1:T(8,128)(2,1)S(1)} collective-permute-done((bf16[2,2,32,4,256]{4,2,3,0,1:T(8,128)(2,1)S(1)}, bf16[2,2,32,4,256]{4,2,3,0,1:T(8,128)(2,1)S(1)}, u32[]{:S(2)}, u32[]{:S(2)}) %collective-permute-start.8) | collective-permute-done | bytes 262176 | tf_op jit(solution)/shard_map/ppermute | solution.py:42
  222.5 3.3 copy.39
  225.8 4.9 %fusion.52 = f32[512,4,2,256]{3,0,2,1:T(8,128)S(1)} fusion(bf16[4,2,256,512]{3,2,1,0:T(8,128)(2,1)S(1)} %bitcast.173), kind=kOutput, calls=%fused_computation.95 | convolution fusion | flops 1078198272 | bytes 6291456 | tf_op jit(solution)/shard_map/dot_general | solution.py:173
  230.7 4.9 %fusion.58 = f32[512,4,2,256]{3,0,2,1:T(8,128)S(1)} fusion(bf16[4,2,256,512]{3,2,1,0:T(8,128)(2,1)S(1)} %bitcast.174), kind=kOutput, calls=%fused_computation.97 | convolution fusion | flops 1077936128 | bytes 6291456 | tf_op jit(solution)/shard_map/dot_general | solution.py:172
  240.3 67.4 %fusion.1 = bf16[512,32,2,256]{3,2,1,0:T(2,128)(2,1)} fusion(bf16[512,32,2,256]{3,2,1,0:T(2,128)(2,1)} %param.6, f32[512,2,256]{2,1,0:T(2,128)S(1)} %copy.43, f32[512,2,256]{2,1,0:T(2,128)S(1)} %copy.42, f32[512,2,256]{2,1,0:T(2,128)S(1)} %copy.41, f32[512,2,256]{2,1,0:T(2,128)S(1)} %copy.40, f32[512,32,256]{2,1,0:T(8,128)} %convert_element_type.183, ...), kind=kLoop, calls=%fused_computation.3 | loop fusion | flops 100663296 | bytes 71303680 | tf_op jit(solution)/shard_map/mul | solution.py:120
  307.7 9.4 %convert_bitcast_fusion = bf16[512,4,2,256]{3,1,2,0:T(4,128)(2,1)} fusion(bf16[512,32,2,256]{3,2,1,0:T(2,128)(2,1)} %fusion.1, f32[32,4]{0,1:T(4,128)S(1)} %copy-done.11), kind=kOutput, calls=%fused_computation.50 | convolution fusion | flops 67108864 | bytes 18874880 | tf_op jit(solution)/shard_map/cs,kczl->kszl/dot_general | solution.py:121
  320.1 4.9 %fusion.13 = f32[512,4,2,256]{3,0,2,1:T(8,128)S(1)} fusion(bf16[512,4,2,256]{0,3,2,1:T(8,128)(2,1)S(1)} %copy.45), kind=kOutput, calls=%fused_computation.40 | convolution fusion | flops 1078198272 | bytes 6291456 | tf_op jit(solution)/shard_map/dot_general | solution.py:100
  325.0 4.9 %fusion.15 = f32[512,4,2,256]{3,0,2,1:T(8,128)S(1)} fusion(bf16[512,4,2,256]{0,3,2,1:T(8,128)(2,1)S(1)} %copy.45), kind=kOutput, calls=%fused_computation.42 | convolution fusion | flops 1077936128 | bytes 6291456 | tf_op jit(solution)/shard_map/dot_general | solution.py:99
  335.4 6.1 %collective-permute-done.11 = bf16[2,2,32,4,256]{4,2,3,0,1:T(8,128)(2,1)S(1)} collective-permute-done((bf16[2,2,32,4,256]{4,2,3,0,1:T(8,128)(2,1)S(1)}, bf16[2,2,32,4,256]{4,2,3,0,1:T(8,128)(2,1)S(1)}, u32[]{:S(2)}, u32[]{:S(2)}) %collective-permute-start.11) | collective-permute-done | bytes 262176 | tf_op jit(solution)/shard_map/ppermute | solution.py:61
  350.4 6.3 %collective-permute-start.14 = (f32[3,4,256]{2,0,1:T(4,128)S(1)}, f32[3,4,256]{2,0,1:T(4,128)S(1)}, u32[]{:S(2)}, u32[]{:S(2)}) collective-permute-start(f32[3,4,256]{2,0,1:T(4,128)S(1)} %get-tuple-element.29), channel_id=1, source_target_pairs={{0,1},{1,2},{2,3},{3,4},{4,5},{5,6},{6,7},{7,8},{8,9},{9,10},{10,1... | collective-permute-start | bytes 36872 | tf_op jit(solution)/shard_map/ppermute | solution.py:19
  358.6 3.1 collective-permute-done.15
  (127 shorter events, 82.5 us)
Async XLA Ops:
  2.3 31.6 %all-to-all-start = ((bf16[16,32,4,256]{3,2,1,0:T(4,128)(2,1)}), bf16[16,32,4,256]{3,2,1,0:T(4,128)(2,1)S(1)}, u32[]{:S(2)}, u32[]{:S(2)}) async-start(bf16[16,32,4,256]{3,2,1,0:T(4,128)(2,1)} %broadcast_in_dim.43), calls=%async_computation | async-start | bytes 2097152 | tf_op jit(solution)/shard_map/all_to_all | solution.py:31
  165.5 2.1 collective-permute-start
  168.9 7.8 %collective-permute-start.1 = (bf16[2,2,32,4,256]{4,2,3,1,0:T(8,128)(2,1)S(1)}, bf16[2,2,32,4,256]{4,2,3,1,0:T(8,128)(2,1)S(1)}, u32[]{:S(2)}, u32[]{:S(2)}) collective-permute-start(bf16[2,2,32,4,256]{4,2,3,1,0:T(8,128)(2,1)S(1)} %fusion.66), channel_id=1, source_target_pairs={{0,2},{1,3},{2,0},{3,1},{4,6},{5,7},{6,4},{7,5},{8,10},{9,11},{10,... | collective-permute-start | bytes 786440 | tf_op jit(solution)/shard_map/ppermute | solution.py:61
  176.9 5.0 %collective-permute-start.2 = (bf16[2,32,4,256]{3,1,2,0:T(8,128)(2,1)S(1)}, bf16[2,32,4,256]{3,1,2,0:T(8,128)(2,1)S(1)}, u32[]{:S(2)}, u32[]{:S(2)}) collective-permute-start(bf16[2,32,4,256]{3,1,2,0:T(8,128)(2,1)S(1)} %fusion.87), channel_id=1, source_target_pairs={{0,4},{1,5},{2,6},{3,7},{4,0},{5,1},{6,2},{7,3},{8,12},{9,13},{10,... | collective-permute-start | bytes 393224 | tf_op jit(solution)/shard_map/ppermute | solution.py:61
  181.9 4.1 %collective-permute-start.3 = (bf16[32,4,256]{2,0,1:T(8,128)(2,1)S(1)}, bf16[32,4,256]{2,0,1:T(8,128)(2,1)S(1)}, u32[]{:S(2)}, u32[]{:S(2)}) collective-permute-start(bf16[32,4,256]{2,0,1:T(8,128)(2,1)S(1)} %fusion.91), channel_id=1, source_target_pairs={{0,8},{1,9},{2,10},{3,11},{4,12},{5,13},{6,14},{7,15},{8,0},{9,1},... | collective-permute-start | bytes 196616 | tf_op jit(solution)/shard_map/ppermute | solution.py:61
  183.9 25.0 %copy-start.4 = (f32[4]{0:T(128)}, f32[4]{0:T(128)S(1)}, u32[]{:S(2)}) copy-start(f32[4]{0:T(128)S(1)} %get-tuple-element.40) | copy-start | bytes 52
  186.0 7.6 %collective-permute-start.4 = (f32[3,4,256]{2,0,1:T(4,128)S(1)}, f32[3,4,256]{2,0,1:T(4,128)S(1)}, u32[]{:S(2)}, u32[]{:S(2)}) collective-permute-start(f32[3,4,256]{2,0,1:T(4,128)S(1)} %get-tuple-element.33), channel_id=1, source_target_pairs={{0,1},{1,2},{2,3},{3,4},{4,5},{5,6},{6,7},{7,8},{8,9},{9,10},{10,1... | collective-permute-start | bytes 36872 | tf_op jit(solution)/shard_map/ppermute | solution.py:19
  191.7 5.1 %collective-permute-start.5 = (f32[3,4,256]{2,0,1:T(4,128)S(1)}, f32[3,4,256]{2,0,1:T(4,128)S(1)}, u32[]{:S(2)}, u32[]{:S(2)}) collective-permute-start(f32[3,4,256]{2,0,1:T(4,128)S(1)} %get-tuple-element.34), channel_id=1, source_target_pairs={{1,0},{2,1},{3,2},{4,3},{5,4},{6,5},{7,6},{8,7},{9,8},{10,9},{11,1... | collective-permute-start | bytes 36872 | tf_op jit(solution)/shard_map/ppermute | solution.py:21
  197.2 4.8 %collective-permute-start.6 = (bf16[32,4,256]{2,0,1:T(8,128)(2,1)S(1)}, bf16[32,4,256]{2,0,1:T(8,128)(2,1)S(1)}, u32[]{:S(2)}, u32[]{:S(2)}) collective-permute-start(bf16[32,4,256]{2,0,1:T(8,128)(2,1)S(1)} %get-tuple-element.5), channel_id=1, source_target_pairs={{0,8},{1,9},{2,10},{3,11},{4,12},{5,13},{6,14},{7,15},{8,0},{9,1},... | collective-permute-start | bytes 196616 | tf_op jit(solution)/shard_map/ppermute | solution.py:42
  202.0 4.1 %collective-permute-start.7 = (bf16[2,32,4,256]{3,1,2,0:T(8,128)(2,1)S(1)}, bf16[2,32,4,256]{3,1,2,0:T(8,128)(2,1)S(1)}, u32[]{:S(2)}, u32[]{:S(2)}) collective-permute-start(bf16[2,32,4,256]{3,1,2,0:T(8,128)(2,1)S(1)} %pad_maximum_fusion.12), channel_id=1, source_target_pairs={{0,4},{1,5},{2,6},{3,7},{4,0},{5,1},{6,2},{7,3},{8,12},{9,13},{10,... | collective-permute-start | bytes 393224 | tf_op jit(solution)/shard_map/ppermute | solution.py:42
  206.2 8.0 %collective-permute-start.8 = (bf16[2,2,32,4,256]{4,2,3,0,1:T(8,128)(2,1)S(1)}, bf16[2,2,32,4,256]{4,2,3,0,1:T(8,128)(2,1)S(1)}, u32[]{:S(2)}, u32[]{:S(2)}) collective-permute-start(bf16[2,2,32,4,256]{4,2,3,0,1:T(8,128)(2,1)S(1)} %pad_maximum_fusion.7), channel_id=1, source_target_pairs={{0,2},{1,3},{2,0},{3,1},{4,6},{5,7},{6,4},{7,5},{8,10},{9,11},{10,... | collective-permute-start | bytes 786440 | tf_op jit(solution)/shard_map/ppermute | solution.py:42
  214.3 3.5 collective-permute-start.9
  240.3 67.4 %copy-start.11 = (f32[32,4]{0,1:T(4,128)S(1)}, f32[32,4]{0,1:T(4,128)}, u32[]{:S(2)}) copy-start(f32[32,4]{0,1:T(4,128)} %param.8) | copy-start | bytes 1540
  331.5 30.3 %copy-start.13 = (pred[36]{0:T(512)(128)(4,1)S(1)}, pred[36]{0:T(512)(128)(4,1)}, u32[]{:S(2)}) copy-start(pred[36]{0:T(512)(128)(4,1)} %copy-done.12) | copy-start | bytes 112
  331.6 30.4 %copy-start.3 = (f32[4]{0:T(128)S(1)}, f32[4]{0:T(128)}, u32[]{:S(2)}) copy-start(f32[4]{0:T(128)} %copy-done.2) | copy-start | bytes 52
  331.6 30.4 %copy-start.5 = (f32[4]{0:T(128)S(1)}, f32[4]{0:T(128)}, u32[]{:S(2)}) copy-start(f32[4]{0:T(128)} %copy-done.4) | copy-start | bytes 52
  331.7 30.4 %copy-start.7 = (f32[4]{0:T(128)S(1)}, f32[4]{0:T(128)}, u32[]{:S(2)}) copy-start(f32[4]{0:T(128)} %copy-done.6) | copy-start | bytes 52
  331.7 30.4 %copy-start.9 = (f32[4]{0:T(128)S(1)}, f32[4]{0:T(128)}, u32[]{:S(2)}) copy-start(f32[4]{0:T(128)} %copy-done.8) | copy-start | bytes 52
  331.7 2.0 collective-permute-start.10
  333.9 7.6 %collective-permute-start.11 = (bf16[2,2,32,4,256]{4,2,3,0,1:T(8,128)(2,1)S(1)}, bf16[2,2,32,4,256]{4,2,3,0,1:T(8,128)(2,1)S(1)}, u32[]{:S(2)}, u32[]{:S(2)}) collective-permute-start(bf16[2,2,32,4,256]{4,2,3,0,1:T(8,128)(2,1)S(1)} %fusion.67), channel_id=1, source_target_pairs={{0,2},{1,3},{2,0},{3,1},{4,6},{5,7},{6,4},{7,5},{8,10},{9,11},{10,... | collective-permute-start | bytes 786440 | tf_op jit(solution)/shard_map/ppermute | solution.py:61
  341.6 4.4 %collective-permute-start.12 = (bf16[2,32,4,256]{3,1,2,0:T(8,128)(2,1)S(1)}, bf16[2,32,4,256]{3,1,2,0:T(8,128)(2,1)S(1)}, u32[]{:S(2)}, u32[]{:S(2)}) collective-permute-start(bf16[2,32,4,256]{3,1,2,0:T(8,128)(2,1)S(1)} %fusion.88), channel_id=1, source_target_pairs={{0,4},{1,5},{2,6},{3,7},{4,0},{5,1},{6,2},{7,3},{8,12},{9,13},{10,... | collective-permute-start | bytes 393224 | tf_op jit(solution)/shard_map/ppermute | solution.py:61
  346.0 4.3 %collective-permute-start.13 = (bf16[32,4,256]{2,0,1:T(8,128)(2,1)S(1)}, bf16[32,4,256]{2,0,1:T(8,128)(2,1)S(1)}, u32[]{:S(2)}, u32[]{:S(2)}) collective-permute-start(bf16[32,4,256]{2,0,1:T(8,128)(2,1)S(1)} %fusion.92), channel_id=1, source_target_pairs={{0,8},{1,9},{2,10},{3,11},{4,12},{5,13},{6,14},{7,15},{8,0},{9,1},... | collective-permute-start | bytes 196616 | tf_op jit(solution)/shard_map/ppermute | solution.py:61
  350.4 8.2 %collective-permute-start.14 = (f32[3,4,256]{2,0,1:T(4,128)S(1)}, f32[3,4,256]{2,0,1:T(4,128)S(1)}, u32[]{:S(2)}, u32[]{:S(2)}) collective-permute-start(f32[3,4,256]{2,0,1:T(4,128)S(1)} %get-tuple-element.29), channel_id=1, source_target_pairs={{0,1},{1,2},{2,3},{3,4},{4,5},{5,6},{6,7},{7,8},{8,9},{9,10},{10,1... | collective-permute-start | bytes 36872 | tf_op jit(solution)/shard_map/ppermute | solution.py:19
  356.7 5.1 %collective-permute-start.15 = (f32[3,4,256]{2,0,1:T(4,128)S(1)}, f32[3,4,256]{2,0,1:T(4,128)S(1)}, u32[]{:S(2)}, u32[]{:S(2)}) collective-permute-start(f32[3,4,256]{2,0,1:T(4,128)S(1)} %get-tuple-element.30), channel_id=1, source_target_pairs={{1,0},{2,1},{3,2},{4,3},{5,4},{6,5},{7,6},{8,7},{9,8},{10,9},{11,1... | collective-permute-start | bytes 36872 | tf_op jit(solution)/shard_map/ppermute | solution.py:21
  (8 other events, 130.7 us)

commit v3 on v1

--- a/solution.py
+++ b/solution.py
@@ -49,8 +49,20 @@
 
 def sum_rows(values, axis):
     count = lax.axis_size(axis)
-    chunks = values.reshape((count, values.shape[0] // count) + values.shape[1:])
-    received = lax.all_to_all(chunks.astype(jnp.bfloat16), axis, 0, 0, tiled=True)
+    half = count // 2
+    parity = lax.axis_index(axis) % 2
+    strip = values.shape[0] // count
+    pairs = values.reshape((half, 2, strip) + values.shape[1:])
+    even = pairs[:, 0]
+    odd = pairs[:, 1]
+    keep = jnp.where(parity == 1, odd, even)
+    send = jnp.where(parity == 1, even, odd)
+    moved = lax.ppermute(
+        send.astype(jnp.bfloat16), axis, [(i, i ^ 1) for i in range(count)]
+    )
+    chip_sum = (keep + moved.astype(jnp.float32)).astype(jnp.bfloat16)
+    groups = [list(range(p, count, 2)) for p in range(2)]
+    received = lax.all_to_all(chip_sum, axis, 0, 0, tiled=True, axis_index_groups=groups)
     return received.astype(jnp.float32).sum(axis=0)
 
 

time: 265 us -> 247 us (0.932)
  blocking collectives: 30.9 us -> 17.2 us
  starting transfers between devices: 33.8 us -> 29.6 us
    all_to_all x1, blocking collectives: 30.9 us -> 17.2 us  [sum_rows(): lax.all_to_all(chip_sum, axis, 0, 0, tiled=True, axis_index_groups=groups)]
    all_to_all x1, waiting for transfers between devices: 23.1 us -> 13.6 us  [sum_rows(): lax.all_to_all(chip_sum, axis, 0, 0, tiled=True, axis_index_groups=groups)]
    ppermute x4, starting transfers between devices: 10.7 us -> 2.86 us  [gather_rows(): lax.ppermute(joined, axis, [(i, i ^ 1 << bit) for i in range(count)])]
    ppermute x4, waiting for transfers between devices: 10.8 us -> 17.2 us  [gather_rows(): lax.ppermute(joined, axis, [(i, i ^ 1 << bit) for i in range(count)])]
    ppermute x2, starting transfers between devices: 5.74 us -> 9.51 us  [padded_2(): lax.ppermute(tail, axis, [(i, (i + 1) % count) for i in range(ends)])]
    ppermute x0 -> x2, waiting for transfers between devices: none -> 3.33 us  [sum_rows(): lax.ppermute(send.astype(jnp.bfloat16), axis, [(i, i ^ 1) for i in range(...]
  transfers between devices with their start and end apart: 10 -> 12, of which waited for: 7 -> 9; matrix products, arithmetic and copies ran while one was open for 9% -> 10% of each run, Pallas kernels for 0% -> 0%
where the time goes in v3:
time: 247 us; the launch traced here: 246 us
  matrix products  91.4 us (37%)
  waiting for transfers between devices  40.4 us (16%)
  local copies, waits for them, and re-layouts  34.4 us (14%)
  other arithmetic  32.2 us (13%)
  starting transfers between devices  29.6 us (12%)
  blocking collectives  17.2 us (7%)
    dot_general x2, matrix products, block_gradient(): summed = jnp.einsum('cs,kczl->kszl', mix_block, weighted)  47.6 us
    ppermute x4, waiting for transfers between devices, gather_rows(): lax.ppermute(joined, axis, [(i, i ^ 1 << bit) for i in range(count)])  17.2 us
    all_to_all x1, blocking collectives, sum_rows(): lax.all_to_all(chip_sum, axis, 0, 0, tiled=True, axis_index_groups=groups)  17.2 us
    convert_element_type x2, local copies, waits for them, and re-layouts, block_gradient(): return summed.astype(jnp.bfloat16)  16 us
    all_to_all x1, waiting for transfers between devices, sum_rows(): lax.all_to_all(chip_sum, axis, 0, 0, tiled=True, axis_index_groups=groups)  13.6 us
    mul x1, other arithmetic, block_gradient(): weighted = weight[None, :, None, None] * beam_gain * residual  11.7 us
    dot_general x2, matrix products, body(): jnp.dot(row_imag, packed, preferred_element_type=jnp.float32)  11.6 us
    convert_element_type x1, other arithmetic, block_gradient(): beam_gain = beam_block.astype(jnp.float32)[:, :, None, :]  11.3 us
  transfers between devices with their start and end apart: 12, of which 9 were waited for; matrix products, arithmetic and copies ran while one was open for 10% of the time, Pallas kernels for 0%

profile of v3, /device:TPU:1, one launch (start us, length us, event | category | flops | bytes accessed | tf_op | source)
XLA Modules:
  0.0 245.8 jit_solution(4815840434881070803)
XLA Ops:
  2.3 7.3 %all-to-all-start = ((bf16[16,32,4,256]{3,2,1,0:T(4,128)(2,1)}), bf16[16,32,4,256]{3,2,1,0:T(4,128)(2,1)S(1)}, u32[]{:S(2)}, u32[]{:S(2)}) async-start(bf16[16,32,4,256]{3,2,1,0:T(4,128)(2,1)} %broadcast_in_dim.43), calls=%async_computation | async-start | bytes 2097152 | tf_op jit(solution)/shard_map/all_to_all | solution.py:31
  9.7 11.3 %convert_element_type.141 = f32[512,32,256]{2,1,0:T(8,128)} convert(bf16[512,32,256]{2,1,0:T(8,128)(2,1)} %param.7) | non-fusion elementwise | flops 4194304 | bytes 25165824 | tf_op jit(solution)/shard_map/convert_element_type | solution.py:115
  22.1 11.7 %broadcast_multiply_fusion = f32[512,32,256]{2,1,0:T(8,128)} fusion(f32[32]{0:T(128)S(1)} %convert_multiply_fusion.1, bf16[512,32,256]{2,1,0:T(8,128)(2,1)} %param.7), kind=kLoop, calls=%fused_computation.16 | loop fusion | flops 8388608 | bytes 25165952 | tf_op jit(solution)/shard_map/mul | solution.py:118
  37.4 3.1 %reshape.88 = bf16[512,2048]{1,0:T(8,128)(2,1)S(1)} reshape(bf16[2048,512]{1,0:T(8,128)(2,1)} %copy.40) | data formatting | bytes 4194304 | tf_op jit(solution)/shard_map/reshape | solution.py:88
  43.3 6.6 %fusion.63 = f32[512,4,2,256]{3,0,2,1:T(8,128)S(1)} fusion(bf16[4,2,256,512]{3,2,1,0:T(8,128)(2,1)} %bitcast.142), kind=kOutput, calls=%fused_computation.82 | convolution fusion | flops 1078198272 | bytes 6291456 | tf_op jit(solution)/shard_map/dot_general | solution.py:171
  50.0 4.9 %fusion.69 = f32[512,4,2,256]{3,0,2,1:T(8,128)S(1)} fusion(bf16[4,2,256,512]{3,2,1,0:T(8,128)(2,1)S(1)} %bitcast.143), kind=kOutput, calls=%fused_computation.84 | convolution fusion | flops 1077936128 | bytes 6291456 | tf_op jit(solution)/shard_map/dot_general | solution.py:170
  56.5 23.7 %convert_bitcast_fusion.1 = bf16[512,4,2,256]{3,1,2,0:T(4,128)(2,1)} fusion(f32[512,32,256]{2,1,0:T(8,128)} %convert_element_type.141, f32[512,32,256]{2,1,0:T(8,128)} %broadcast_multiply_fusion, bf16[512,32,2,256]{3,2,1,0:T(2,128)(2,1)} %param.6, bf16[512,4,2,256]{3,0,2,1:T(8,128)(2,1)S(1)} %pad_maximum_fusion, f32[32,4]{0,1:T(4,128)S(1)} %copy-done.2), kind=kOutput, calls=%fused_computation.51 | convolution fusion | flops 176160896 | bytes 54526464 | tf_op jit(solution)/shard_map/cs,kczl->kszl/dot_general | solution.py:119
  80.2 13.0 %copy.44 = bf16[512,4,2,256]{0,3,2,1:T(8,128)(2,1)S(1)} copy(bf16[512,4,2,256]{3,1,2,0:T(4,128)(2,1)} %convert_bitcast_fusion.1) | data formatting | bytes 4194304 | tf_op jit(solution)/shard_map/convert_element_type | solution.py:120
  93.2 4.9 %fusion.33 = f32[512,4,2,256]{3,0,2,1:T(8,128)S(1)} fusion(bf16[512,4,2,256]{0,3,2,1:T(8,128)(2,1)S(1)} %copy.44), kind=kOutput, calls=%fused_computation.46 | convolution fusion | flops 1078198272 | bytes 6291456 | tf_op jit(solution)/shard_map/dot_general | solution.py:101
  98.1 4.9 %fusion.35 = f32[512,4,2,256]{3,0,2,1:T(8,128)S(1)} fusion(bf16[512,4,2,256]{0,3,2,1:T(8,128)(2,1)S(1)} %copy.44), kind=kOutput, calls=%fused_computation.48 | convolution fusion | flops 1077936128 | bytes 6291456 | tf_op jit(solution)/shard_map/dot_general | solution.py:100
  107.9 5.4 %all-to-all-start.1 = ((bf16[8,32,4,256]{3,1,2,0:T(8,128)(2,1)}), bf16[8,32,4,256]{3,1,2,0:T(8,128)(2,1)S(1)}, u32[]{:S(2)}, u32[]{:S(2)}) async-start(bf16[8,32,4,256]{3,1,2,0:T(8,128)(2,1)} %fusion.50), calls=%async_computation.1 | async-start | bytes 1048576 | tf_op jit(solution)/shard_map/all_to_all | solution.py:65
  113.3 13.6 %all-to-all-done.1 = bf16[8,32,4,256]{3,1,2,0:T(8,128)(2,1)S(1)} async-done(((bf16[8,32,4,256]{3,1,2,0:T(8,128)(2,1)}), bf16[8,32,4,256]{3,1,2,0:T(8,128)(2,1)S(1)}, u32[]{:S(2)}, u32[]{:S(2)}) %all-to-all-start.1) | async-done | bytes 524320 | tf_op jit(solution)/shard_map/all_to_all | solution.py:65
  127.0 4.8 %collective-permute-start.1 = (f32[3,4,256]{2,0,1:T(4,128)S(1)}, f32[3,4,256]{2,0,1:T(4,128)S(1)}, u32[]{:S(2)}, u32[]{:S(2)}) collective-permute-start(f32[3,4,256]{2,0,1:T(4,128)S(1)} %get-tuple-element.25), channel_id=1, source_target_pairs={{0,1},{1,2},{2,3},{3,4},{4,5},{5,6},{6,7},{7,8},{8,9},{9,10},{10,1... | collective-permute-start | bytes 36872 | tf_op jit(solution)/shard_map/ppermute | solution.py:19
  137.5 4.7 %collective-permute-done.3 = bf16[32,4,256]{2,0,1:T(8,128)(2,1)S(1)} collective-permute-done((bf16[32,4,256]{2,0,1:T(8,128)(2,1)S(1)}, bf16[32,4,256]{2,0,1:T(8,128)(2,1)S(1)}, u32[]{:S(2)}, u32[]{:S(2)}) %collective-permute-start.3) | collective-permute-done | bytes 65568 | tf_op jit(solution)/shard_map/ppermute | solution.py:42
  142.3 4.9 %collective-permute-done.4 = bf16[2,32,4,256]{3,1,2,0:T(8,128)(2,1)S(1)} collective-permute-done((bf16[2,32,4,256]{3,1,2,0:T(8,128)(2,1)S(1)}, bf16[2,32,4,256]{3,1,2,0:T(8,128)(2,1)S(1)}, u32[]{:S(2)}, u32[]{:S(2)}) %collective-permute-start.4) | collective-permute-done | bytes 131104 | tf_op jit(solution)/shard_map/ppermute | solution.py:42
  148.4 6.1 %collective-permute-done.5 = bf16[2,2,32,4,256]{4,2,3,0,1:T(8,128)(2,1)S(1)} collective-permute-done((bf16[2,2,32,4,256]{4,2,3,0,1:T(8,128)(2,1)S(1)}, bf16[2,2,32,4,256]{4,2,3,0,1:T(8,128)(2,1)S(1)}, u32[]{:S(2)}, u32[]{:S(2)}) %collective-permute-start.5) | collective-permute-done | bytes 262176 | tf_op jit(solution)/shard_map/ppermute | solution.py:42
  165.7 4.9 %fusion.60 = f32[512,4,2,256]{3,0,2,1:T(8,128)S(1)} fusion(bf16[4,2,256,512]{3,2,1,0:T(8,128)(2,1)S(1)} %bitcast.144), kind=kOutput, calls=%fused_computation.81 | convolution fusion | flops 1078198272 | bytes 6291456 | tf_op jit(solution)/shard_map/dot_general | solution.py:171
  170.6 4.9 %fusion.66 = f32[512,4,2,256]{3,0,2,1:T(8,128)S(1)} fusion(bf16[4,2,256,512]{3,2,1,0:T(8,128)(2,1)S(1)} %bitcast.145), kind=kOutput, calls=%fused_computation.83 | convolution fusion | flops 1077936128 | bytes 6291456 | tf_op jit(solution)/shard_map/dot_general | solution.py:170
  176.6 23.9 %convert_bitcast_fusion = bf16[512,4,2,256]{3,1,2,0:T(4,128)(2,1)} fusion(f32[512,32,256]{2,1,0:T(8,128)} %convert_element_type.141, f32[512,32,256]{2,1,0:T(8,128)} %broadcast_multiply_fusion, bf16[512,32,2,256]{3,2,1,0:T(2,128)(2,1)} %param.6, bf16[512,4,2,256]{3,0,2,1:T(8,128)(2,1)S(1)} %pad_maximum_fusion.1, f32[32,4]{0,1:T(4,128)S(1)} %copy-done.2), kind=kOutput, calls=%fused_computation.50 | convolution fusion | flops 176160896 | bytes 54526464 | tf_op jit(solution)/shard_map/cs,kczl->kszl/dot_general | solution.py:119
  203.5 4.9 %fusion.27 = f32[512,4,2,256]{3,0,2,1:T(8,128)S(1)} fusion(bf16[512,4,2,256]{0,3,2,1:T(8,128)(2,1)S(1)} %copy.55), kind=kOutput, calls=%fused_computation.40 | convolution fusion | flops 1078198272 | bytes 6291456 | tf_op jit(solution)/shard_map/dot_general | solution.py:101
  208.4 4.9 %fusion.29 = f32[512,4,2,256]{3,0,2,1:T(8,128)S(1)} fusion(bf16[512,4,2,256]{0,3,2,1:T(8,128)(2,1)S(1)} %copy.55), kind=kOutput, calls=%fused_computation.42 | convolution fusion | flops 1077936128 | bytes 6291456 | tf_op jit(solution)/shard_map/dot_general | solution.py:100
  217.3 17.2 %all_to_all.15 = bf16[8,32,4,256]{3,1,2,0:T(8,128)(2,1)S(1)} all-to-all(bf16[8,32,4,256]{3,1,2,0:T(8,128)(2,1)S(1)} %fusion.51), channel_id=1, replica_groups={{0,2,4,6,8,10,12,14},{1,3,5,7,9,11,13,15},{16,18,20,22,24,26,28,30},{17..., dimensions={0} | all-to-all | bytes 1048576 | tf_op jit(solution)/shard_map/all_to_all | solution.py:65
  234.6 4.7 %collective-permute-start.8 = (f32[3,4,256]{2,0,1:T(4,128)S(1)}, f32[3,4,256]{2,0,1:T(4,128)S(1)}, u32[]{:S(2)}, u32[]{:S(2)}) collective-permute-start(f32[3,4,256]{2,0,1:T(4,128)S(1)} %get-tuple-element.21), channel_id=1, source_target_pairs={{0,1},{1,2},{2,3},{3,4},{4,5},{5,6},{6,7},{7,8},{8,9},{9,10},{10,1... | collective-permute-start | bytes 36872 | tf_op jit(solution)/shard_map/ppermute | solution.py:19
  241.3 3.1 %collective-permute-done.9 = f32[3,4,256]{2,0,1:T(4,128)S(1)} collective-permute-done((f32[3,4,256]{2,0,1:T(4,128)S(1)}, f32[3,4,256]{2,0,1:T(4,128)S(1)}, u32[]{:S(2)}, u32[]{:S(2)}) %collective-permute-start.9) | collective-permute-done | bytes 12320 | tf_op jit(solution)/shard_map/ppermute | solution.py:21
  (87 shorter events, 45.7 us)
Async XLA Ops:
  2.3 31.5 %all-to-all-start = ((bf16[16,32,4,256]{3,2,1,0:T(4,128)(2,1)}), bf16[16,32,4,256]{3,2,1,0:T(4,128)(2,1)S(1)}, u32[]{:S(2)}, u32[]{:S(2)}) async-start(bf16[16,32,4,256]{3,2,1,0:T(4,128)(2,1)} %broadcast_in_dim.43), calls=%async_computation | async-start | bytes 2097152 | tf_op jit(solution)/shard_map/all_to_all | solution.py:31
  9.7 12.4 %copy-start.8 = (s32[32]{0:T(128)S(1)}, s32[32]{0:T(128)}, u32[]{:S(2)}) copy-start(s32[32]{0:T(128)} %param.9) | copy-start | bytes 388
  43.3 6.7 %copy-start = (bf16[2048,512]{1,0:T(8,128)(2,1)S(1)}, bf16[2048,512]{1,0:T(8,128)(2,1)}, u32[]{:S(2)}) copy-start(bf16[2048,512]{1,0:T(8,128)(2,1)} %copy.71) | copy-start | bytes 6291460
  55.8 0.7 copy-start.2
  104.8 8.5 %copy-start.7 = (s32[4,2]{0,1:T(2,128)S(1)}, s32[4,2]{0,1:T(2,128)}, u32[]{:S(2)}) copy-start(s32[4,2]{0,1:T(2,128)} %param.10) | copy-start | bytes 100
  104.8 22.2 %copy-start.1 = (f32[32,4,256]{2,1,0:T(4,128)S(1)}, f32[32,4,256]{2,1,0:T(4,128)}, u32[]{:S(2)}) copy-start(f32[32,4,256]{2,1,0:T(4,128)} %param.11) | copy-start | bytes 393220
  104.8 2.0 collective-permute-start
  107.9 19.0 %all-to-all-start.1 = ((bf16[8,32,4,256]{3,1,2,0:T(8,128)(2,1)}), bf16[8,32,4,256]{3,1,2,0:T(8,128)(2,1)S(1)}, u32[]{:S(2)}, u32[]{:S(2)}) async-start(bf16[8,32,4,256]{3,1,2,0:T(8,128)(2,1)} %fusion.50), calls=%async_computation.1 | async-start | bytes 1048576 | tf_op jit(solution)/shard_map/all_to_all | solution.py:65
  113.3 24.1 %copy-start.3 = (f32[4]{0:T(128)}, f32[4]{0:T(128)S(1)}, u32[]{:S(2)}) copy-start(f32[4]{0:T(128)S(1)} %get-tuple-element.30) | copy-start | bytes 52
  127.0 6.7 %collective-permute-start.1 = (f32[3,4,256]{2,0,1:T(4,128)S(1)}, f32[3,4,256]{2,0,1:T(4,128)S(1)}, u32[]{:S(2)}, u32[]{:S(2)}) collective-permute-start(f32[3,4,256]{2,0,1:T(4,128)S(1)} %get-tuple-element.25), channel_id=1, source_target_pairs={{0,1},{1,2},{2,3},{3,4},{4,5},{5,6},{6,7},{7,8},{8,9},{9,10},{10,1... | collective-permute-start | bytes 36872 | tf_op jit(solution)/shard_map/ppermute | solution.py:19
  131.8 5.1 %collective-permute-start.2 = (f32[3,4,256]{2,0,1:T(4,128)S(1)}, f32[3,4,256]{2,0,1:T(4,128)S(1)}, u32[]{:S(2)}, u32[]{:S(2)}) collective-permute-start(f32[3,4,256]{2,0,1:T(4,128)S(1)} %get-tuple-element.26), channel_id=1, source_target_pairs={{1,0},{2,1},{3,2},{4,3},{5,4},{6,5},{7,6},{8,7},{9,8},{10,9},{11,1... | collective-permute-start | bytes 36872 | tf_op jit(solution)/shard_map/ppermute | solution.py:21
  133.8 3.4 %copy-start.5 = (pred[36]{0:T(512)(128)(4,1)}, pred[36]{0:T(512)(128)(4,1)S(1)}, u32[]{:S(2)}) copy-start(pred[36]{0:T(512)(128)(4,1)S(1)} %compare_and_fusion) | copy-start | bytes 112
  137.4 4.8 %collective-permute-start.3 = (bf16[32,4,256]{2,0,1:T(8,128)(2,1)S(1)}, bf16[32,4,256]{2,0,1:T(8,128)(2,1)S(1)}, u32[]{:S(2)}, u32[]{:S(2)}) collective-permute-start(bf16[32,4,256]{2,0,1:T(8,128)(2,1)S(1)} %get-tuple-element.5), channel_id=1, source_target_pairs={{0,8},{1,9},{2,10},{3,11},{4,12},{5,13},{6,14},{7,15},{8,0},{9,1},... | collective-permute-start | bytes 196616 | tf_op jit(solution)/shard_map/ppermute | solution.py:42
  142.2 5.0 %collective-permute-start.4 = (bf16[2,32,4,256]{3,1,2,0:T(8,128)(2,1)S(1)}, bf16[2,32,4,256]{3,1,2,0:T(8,128)(2,1)S(1)}, u32[]{:S(2)}, u32[]{:S(2)}) collective-permute-start(bf16[2,32,4,256]{3,1,2,0:T(8,128)(2,1)S(1)} %pad_maximum_fusion.15), channel_id=1, source_target_pairs={{0,4},{1,5},{2,6},{3,7},{4,0},{5,1},{6,2},{7,3},{8,12},{9,13},{10,... | collective-permute-start | bytes 393224 | tf_op jit(solution)/shard_map/ppermute | solution.py:42
  147.2 7.3 %collective-permute-start.5 = (bf16[2,2,32,4,256]{4,2,3,0,1:T(8,128)(2,1)S(1)}, bf16[2,2,32,4,256]{4,2,3,0,1:T(8,128)(2,1)S(1)}, u32[]{:S(2)}, u32[]{:S(2)}) collective-permute-start(bf16[2,2,32,4,256]{4,2,3,0,1:T(8,128)(2,1)S(1)} %pad_maximum_fusion.8), channel_id=1, source_target_pairs={{0,2},{1,3},{2,0},{3,1},{4,6},{5,7},{6,4},{7,5},{8,10},{9,11},{10,... | collective-permute-start | bytes 786440 | tf_op jit(solution)/shard_map/ppermute | solution.py:42
  154.6 3.1 %collective-permute-start.6 = (bf16[2,2,2,32,4,256]{5,3,4,0,1,2:T(8,128)(2,1)S(1)}, bf16[2,2,2,32,4,256]{5,3,4,0,1,2:T(8,128)(2,1)S(1)}, u32[]{:S(2)}, u32[]{:S(2)}) collective-permute-start(bf16[2,2,2,32,4,256]{5,3,4,0,1,2:T(8,128)(2,1)S(1)} %pad_maximum_fusion.5), channel_id=1, source_target_pairs={{0,1},{1,0},{2,3},{3,2},{4,5},{5,4},{6,7},{7,6},{8,9},{9,8},{10,11... | collective-permute-start | bytes 1572872 | tf_op jit(solution)/shard_map/ppermute | solution.py:42
  215.0 2.0 collective-permute-start.7
  217.3 27.2 %copy-start.6 = (pred[36]{0:T(512)(128)(4,1)S(1)}, pred[36]{0:T(512)(128)(4,1)}, u32[]{:S(2)}) copy-start(pred[36]{0:T(512)(128)(4,1)} %copy-done.5) | copy-start | bytes 112
  217.3 27.4 %copy-start.4 = (f32[4]{0:T(128)S(1)}, f32[4]{0:T(128)}, u32[]{:S(2)}) copy-start(f32[4]{0:T(128)} %copy-done.3) | copy-start | bytes 52
  234.6 6.7 %collective-permute-start.8 = (f32[3,4,256]{2,0,1:T(4,128)S(1)}, f32[3,4,256]{2,0,1:T(4,128)S(1)}, u32[]{:S(2)}, u32[]{:S(2)}) collective-permute-start(f32[3,4,256]{2,0,1:T(4,128)S(1)} %get-tuple-element.21), channel_id=1, source_target_pairs={{0,1},{1,2},{2,3},{3,4},{4,5},{5,6},{6,7},{7,8},{8,9},{9,10},{10,1... | collective-permute-start | bytes 36872 | tf_op jit(solution)/shard_map/ppermute | solution.py:19
  239.4 5.1 %collective-permute-start.9 = (f32[3,4,256]{2,0,1:T(4,128)S(1)}, f32[3,4,256]{2,0,1:T(4,128)S(1)}, u32[]{:S(2)}, u32[]{:S(2)}) collective-permute-start(f32[3,4,256]{2,0,1:T(4,128)S(1)} %get-tuple-element.22), channel_id=1, source_target_pairs={{1,0},{2,1},{3,2},{4,3},{5,4},{6,5},{7,6},{8,7},{9,8},{10,9},{11,1... | collective-permute-start | bytes 36872 | tf_op jit(solution)/shard_map/ppermute | solution.py:21
